TPU v7x, 128 devices: a whole 4x4x4 slice. The times are simulated.
128 devices in a mesh: seq: 16 (over y, z), row: 2 (over core), col: 4 (over x).
Axes of the slice: x: 4, y: 4, z: 4, core: 2. Of those that a mesh axis runs over, the one named last changes fastest.
Arguments:
- hidden_in: bfloat16 [256, 1536], P('seq'), may hold values from -40 to 40
- attn_gain: float32 [1536], replicated, may hold values from 0.25 to 1.75
- w_query: bfloat16 [1536, 1536], P('seq', ('row', 'col')), may hold values from -0.15625 to 0.15625
- w_keyval: bfloat16 [1536, 1024], P('seq', ('row', 'col')), may hold values from -0.15625 to 0.15625
- w_out: bfloat16 [1536, 1536], P(('row', 'col'), 'seq'), may hold values from -0.15625 to 0.15625
- kv_cache: bfloat16 [64, 24576, 1024], P(None, 'seq', ('row', 'col')), may hold values from -360 to 360
- cache_len: int32 [64], replicated, may hold values from 1 to 24576, as said below
- ffn_gain: float32 [1536], replicated, may hold values from 0.25 to 1.75
- w_router: float32 [1536, 16], replicated, may hold values from -0.15625 to 0.15625
- routes: int32 [256, 2], replicated, may hold values from 0 to 15, all different within a row; in each aligned block of 256 rows (0 to 255, 256 to 511, ...) at most 64 rows name the same one
- w_gate_up: bfloat16 [16, 1536, 2, 1024], P('seq', 'row', None, 'col'), may hold values from -0.15625 to 0.15625
- w_down: bfloat16 [16, 1024, 1536], P('seq', 'col', 'row'), may hold values from -0.1875 to 0.1875
- final_gain: float32 [1536], replicated, may hold values from 0.25 to 1.75
- w_head: bfloat16 [1536, 65536], P('row', ('seq', 'col')), may hold values from -1.75 to 1.75
- targets: int32 [256], replicated, may hold values from 0 to 65535
Outputs:
- layer_out: bfloat16 [256, 1536], P(('seq', 'col'), 'row')
- logprob: float32 [256], replicated
Inputs may be any that keep to these rules, and one draw needn't show every extreme that they name: `cache_len`: lengths are uneven; some request has exactly 24576 cached positions. `routes`: the two experts of a row differ; each expert is named by at most 64 rows, a bound that some block reaches.
All inputs are finite; a program needn't handle non-finite values.
Results may differ from a plain program's by a relative error of at most 0.0044.
Values may be sent and summed in bfloat16 or wider, within the bound.
No kernel may reach another device: no remote copies, remote signals or barrier semaphores. Data moves between devices by JAX's collectives and lax.ppermute only.
A program may use at most 128 MiB of HBM per device.

v0:
```python
import jax
import jax.numpy as jnp
from jax import lax
from jax.sharding import PartitionSpec as P

HD = 64
EXP_DEV = 1
TOP = 2
NEW = 4


EPSILON = 1e-05
NEG_LARGE = -1e30


def combined_all(shard, axis, combine):
    everything = jax.tree.map(lambda part: lax.all_gather(part, axis), shard)
    initial = jax.tree.map(lambda part: part[0], everything)

    def lap(k, so_far):
        return combine(so_far, jax.tree.map(lambda part: part[k], everything))

    return lax.fori_loop(1, lax.axis_size(axis), lap, initial)


def butterfly_merge(value, axes, count, combine):
    widths = [part.shape[-1] for part in value]
    edges = [0]
    for width in widths:
        edges.append(edges[-1] + width)

    def split(packed):
        return tuple(packed[..., edges[i] : edges[i + 1]] for i in range(len(widths)))

    packed = jnp.concatenate(value, axis=-1)
    step = 1
    while step < count:
        pairs = [(i, i ^ step) for i in range(count)]
        other = lax.ppermute(packed, axes, pairs)
        packed = jnp.concatenate(combine(split(packed), split(other)), axis=-1)
        step *= 2
    return split(packed)


def halving_scatter(value, axes, count):
    index = lax.axis_index(axes)
    step = count // 2
    while step >= 1:
        half = value.shape[0] // 2
        upper = (index // step) % 2 == 1
        low, high = value[:half], value[half:]
        send = jnp.where(upper, low, high)
        keep = jnp.where(upper, high, low)
        pairs = [(i, i ^ step) for i in range(count)]
        value = keep + lax.ppermute(send, axes, pairs)
        step //= 2
    return value


def doubling_gather(value, axes, count):
    index = lax.axis_index(axes)
    step = 1
    while step < count:
        upper = (index // step) % 2 == 1
        pairs = [(i, i ^ step) for i in range(count)]
        other = lax.ppermute(value, axes, pairs)
        value = jnp.where(
            upper, jnp.concatenate([other, value]), jnp.concatenate([value, other])
        )
        step *= 2
    return value


def merge_logsumexp(first, second):
    high_a, sums_a, picked_a = first
    high_b, sums_b, picked_b = second
    highest = jnp.maximum(high_a, high_b)
    return (
        highest,
        sums_a * jnp.exp(high_a - highest) + sums_b * jnp.exp(high_b - highest),
        picked_a + picked_b,
    )


def rms_scale(values, gain):
    mean_square = jnp.mean(values * values, axis=-1, keepdims=True)
    return values * lax.rsqrt(mean_square + EPSILON) * gain


def final_scale(state, gain_half, width):
    squares = lax.psum(jnp.sum(state * state, axis=-1), "row")
    return (state * lax.rsqrt(squares[:, None] / width + EPSILON) * gain_half).astype(jnp.bfloat16)


def merge_softmax(first, second):
    high_a, sums_a, mixed_a = first
    high_b, sums_b, mixed_b = second
    highest = jnp.maximum(high_a, high_b)
    factor_a = jnp.exp(high_a - highest)
    factor_b = jnp.exp(high_b - highest)
    shaped_a = mixed_a.reshape(highest.shape + (-1,)) * factor_a[..., None]
    shaped_b = mixed_b.reshape(highest.shape + (-1,)) * factor_b[..., None]
    return (
        highest,
        sums_a * factor_a + sums_b * factor_b,
        (shaped_a + shaped_b).reshape(mixed_a.shape),
    )


def on_device(
    hidden_in,
    attn_gain,
    w_query,
    w_keyval,
    w_out,
    kv_cache,
    cache_len,
    ffn_gain,
    w_router,
    routes,
    w_gate_up,
    w_down,
    final_gain,
    w_head,
    targets,
):
    seq_count = lax.axis_size("seq")
    seq_index = lax.axis_index("seq")
    col_index = lax.axis_index("col")
    row_index = lax.axis_index("row")
    block_index = lax.axis_index(("seq", "col"))
    own_count = hidden_in.shape[0]
    block_start = seq_index * own_count
    pieces = [hidden_in.reshape(-1), w_query.reshape(-1), w_keyval.reshape(-1), w_out.reshape(-1)]
    bounds = [0]
    for piece in pieces:
        bounds.append(bounds[-1] + piece.shape[0])
    packed = lax.all_gather(jnp.concatenate(pieces), "seq", axis=0, tiled=False)
    shards = packed.shape[0]
    every_row = packed[:, bounds[0] : bounds[1]].reshape((-1,) + hidden_in.shape[1:])
    w_query_all = packed[:, bounds[1] : bounds[2]].reshape((-1,) + w_query.shape[1:])
    w_keyval_all = packed[:, bounds[2] : bounds[3]].reshape((-1,) + w_keyval.shape[1:])
    w_out_all = (
        packed[:, bounds[3] : bounds[4]]
        .reshape((shards,) + w_out.shape)
        .transpose(1, 0, 2)
        .reshape(w_out.shape[0], -1)
    )
    total_rows = every_row.shape[0]
    requests = total_rows // NEW
    width = every_row.shape[1]
    half = width // lax.axis_size("row")
    col_start = row_index * half
    state_in = every_row.astype(jnp.float32)
    normed_in = rms_scale(state_in, attn_gain).astype(jnp.bfloat16)
    query_cols = w_query.shape[1]
    group = query_cols // HD
    query = jnp.dot(
        normed_in,
        w_query_all,
        preferred_element_type=jnp.float32,
    )
    fresh_kv = jnp.dot(
        normed_in,
        w_keyval_all,
        preferred_element_type=jnp.float32,
    )
    fresh_kv = fresh_kv.astype(jnp.bfloat16).reshape(requests, NEW, 2, HD)
    queries = query.reshape(requests, NEW * group, HD)
    scale = HD ** (-0.5)
    length_dev = kv_cache.shape[1]
    cached = kv_cache.reshape(requests, length_dev, 2, HD)
    cached_keys = cached[:, :, 0].astype(jnp.float32)
    cached_values = cached[:, :, 1].astype(jnp.float32)
    old_scores = (
        jnp.einsum("rqd,rpd->rqp", queries, cached_keys, precision=lax.Precision.HIGHEST) * scale
    )
    positions = seq_index * length_dev + jnp.arange(length_dev, dtype=jnp.int32)
    old_mask = (positions[None, :] < cache_len[:, None])[:, None, :]
    fresh_keys = fresh_kv[:, :, 0].astype(jnp.float32)
    fresh_values = fresh_kv[:, :, 1].astype(jnp.float32)
    new_scores = (
        jnp.einsum("rqd,rud->rqu", queries, fresh_keys, precision=lax.Precision.HIGHEST) * scale
    )
    token_of = jnp.arange(NEW * group, dtype=jnp.int32) // group
    new_mask = (
        (token_of[:, None] >= jnp.arange(NEW, dtype=jnp.int32)[None, :]) & (seq_index == 0)
    )[None]
    old_scores = jnp.where(old_mask, old_scores, NEG_LARGE)
    new_scores = jnp.where(new_mask, new_scores, NEG_LARGE)
    highest = jnp.maximum(jnp.max(old_scores, axis=-1), jnp.max(new_scores, axis=-1))
    old_weights = jnp.where(old_mask, jnp.exp(old_scores - highest[..., None]), 0.0)
    new_weights = jnp.where(new_mask, jnp.exp(new_scores - highest[..., None]), 0.0)
    totals = old_weights.sum(-1) + new_weights.sum(-1)
    mixed = jnp.einsum("rqp,rpd->rqd", old_weights, cached_values, precision=lax.Precision.HIGHEST)
    mixed = mixed + jnp.einsum(
        "rqu,rud->rqd", new_weights, fresh_values, precision=lax.Precision.HIGHEST
    )
    highest, totals, mixed = butterfly_merge(
        (highest, totals, mixed.reshape(requests, -1)), "seq", seq_count, merge_softmax
    )
    attended = mixed.reshape(requests, NEW * group, HD) / totals[..., None]
    attn_mix = attended.reshape(total_rows, query_cols).astype(jnp.bfloat16)
    partial_out = jnp.dot(
        attn_mix,
        w_out_all,
        preferred_element_type=jnp.float32,
    )
    state_mid = state_in + lax.psum(partial_out, ("row", "col"))
    own_mid = lax.dynamic_slice_in_dim(state_mid, block_start, own_count, 0)
    normed_mid = rms_scale(state_mid, ffn_gain).astype(jnp.bfloat16)
    router = jnp.dot(normed_mid.astype(jnp.float32), w_router, precision=lax.Precision.HIGHEST)
    chosen = jnp.take_along_axis(router, routes, axis=1)
    probs = jax.nn.sigmoid(chosen - chosen[:, ::-1])
    capacity = 2 * total_rows * TOP // (EXP_DEV * seq_count)
    row_ids = jnp.arange(total_rows, dtype=jnp.int32)
    slot_ids = jnp.arange(capacity, dtype=jnp.int32)
    expert = seq_index * EXP_DEV + 0
    member = routes == expert
    in_row = jnp.any(member, axis=1)
    weight_row = jnp.sum(jnp.where(member, probs, 0.0), axis=1)
    ordering = jnp.cumsum(in_row.astype(jnp.int32)) - 1
    filled = jnp.sum(in_row.astype(jnp.int32))
    source = (
        jnp.zeros((capacity,), jnp.int32)
        .at[jnp.where(in_row, ordering, capacity)]
        .set(row_ids, mode="drop")
    )
    source_list = [source]
    weight_list = [jnp.where(slot_ids < filled, weight_row[source], 0.0)]
    source_all = jnp.stack(source_list)
    weight_all = jnp.stack(weight_list)
    normed_half = lax.dynamic_slice_in_dim(normed_mid, col_start, half, 1)
    expert_rows = normed_half[source_all]
    gate_part = jnp.einsum(
        "ecd,edgf->ecgf", expert_rows, w_gate_up, preferred_element_type=jnp.float32
    )
    gate_both = lax.psum(gate_part, "row")
    expert_hidden = (jax.nn.silu(gate_both[:, :, 0]) * gate_both[:, :, 1]).astype(jnp.bfloat16)
    expert_result = jnp.einsum(
        "ecf,efd->ecd", expert_hidden, w_down, preferred_element_type=jnp.float32
    )
    weighted = (expert_result * weight_all[..., None]).reshape(-1, half)
    term = jnp.zeros((total_rows, half), jnp.float32).at[source_all.reshape(-1)].add(weighted)
    block_count = seq_count * lax.axis_size("col")
    out_count = total_rows // block_count
    block_mid = lax.dynamic_slice_in_dim(
        lax.dynamic_slice_in_dim(state_mid, block_index * out_count, out_count, 0), col_start, half, 1
    )
    state_out = halving_scatter(term, ("seq", "col"), block_count) + block_mid
    layer_out = state_out.astype(jnp.bfloat16)
    gain_half = lax.dynamic_slice_in_dim(final_gain, col_start, half, 0)
    normed_block = final_scale(state_out, gain_half, width)
    normed_out = doubling_gather(normed_block, ("seq", "col"), block_count)
    vocab_dev = w_head.shape[1]
    row_count = total_rows // lax.axis_size("row")
    logits = lax.psum_scatter(
        jnp.dot(normed_out, w_head, preferred_element_type=jnp.float32),
        "row",
        scatter_dimension=0,
        tiled=True,
    )
    own_targets = lax.dynamic_slice_in_dim(targets, row_index * row_count, row_count, 0)
    vocab_start = block_index * vocab_dev
    matches = (
        own_targets[:, None] == (vocab_start + jnp.arange(vocab_dev, dtype=jnp.int32))[None, :]
    )
    picked_local = jnp.sum(jnp.where(matches, logits, 0.0), axis=1)
    local_high = jnp.max(logits, axis=1)
    local_total = jnp.sum(jnp.exp(logits - local_high[:, None]), axis=1)
    row_high, row_total, picked = butterfly_merge(
        (local_high[None], local_total[None], picked_local[None]),
        ("seq", "col"),
        seq_count * lax.axis_size("col"),
        merge_logsumexp,
    )
    row_high, row_total, picked = row_high[0], row_total[0], picked[0]
    logprob_part = picked - (row_high + jnp.log(row_total))
    logprob = lax.all_gather(logprob_part, "row", axis=0, tiled=True)
    return (layer_out, logprob)


def solution(mesh):
    return jax.shard_map(
        on_device,
        mesh=mesh,
        in_specs=(
            P("seq", None),
            P(),
            P("seq", ("row", "col")),
            P("seq", ("row", "col")),
            P(("row", "col"), "seq"),
            P(None, "seq", ("row", "col")),
            P(),
            P(),
            P(),
            P(),
            P("seq", "row", None, "col"),
            P("seq", "col", "row"),
            P(),
            P("row", ("seq", "col")),
            P(),
        ),
        out_specs=(P(("seq", "col"), "row"), P()),
        check_vma=False,
    )
```

profile of v0, /device:TPU:1, one launch (start us, length us, event | category | flops | bytes accessed | tf_op | source)
XLA Modules:
  0.0 396.7 jit_solution(7022238766277340115)
XLA Ops:
  10.1 1.4 pad_maximum_fusion.4
  12.9 31.0 %copy.74 = bf16[64,1536,128]{1,2,0:T(8,128)(2,1)} copy(bf16[64,1536,128]{2,1,0:T(8,128)(2,1)} %param.20) | data formatting | bytes 50331648 | tf_op args[5]
  44.7 14.5 %all-gather.4.cloned.1.call-done = bf16[1179648]{0:T(1024)(128)(2,1)} async-done(((bf16[73728]{0:T(1024)(128)(2,1)}), bf16[1179648]{0:T(1024)(128)(2,1)}) %all-gather.4.cloned.1.call-update) | async-done | bytes 2359312 | tf_op jit(solution)/shard_map/all_gather | solution.py:138
  59.2 3.3 reshape.359
  62.5 2.4 slice_convert_fusion
  64.9 2.4 fusion.57
  67.3 1.7 reshape.320
  70.3 2.3 multiply_convert_fusion.1
  72.7 2.4 convert_element_type.65
  75.0 2.9 reshape.300
  77.9 2.5 fusion.60
  80.4 1.8 reshape.301
  83.2 1.6 convolution_convert_fusion
  85.1 1.6 fusion.59
  86.7 10.0 %fusion.2 = (f32[64,12]{1,0:T(8,128)S(1)}, f32[64,12,1536]{2,1,0:T(8,128)S(1)}) fusion(pred[64,1536]{1,0:T(8,128)(4,1)} %broadcast_compare_fusion, f32[64,12,64]{2,1,0:T(8,128)} %reshape.301, bf16[64,1536,2,64]{1,3,2,0:T(8,128)(2,1)} %bitcast.65), kind=kOutput, calls=%fused_computation.11 | convolution fusion | flops 909507840 | bytes 17927168 | tf_op jit(solution)/shard_map/rqd,rpd->rqp/dot_general | solution.py:176
  96.8 13.1 %fusion = f32[64,12,64]{2,1,0:T(8,128)S(1)} fusion(bf16[64,1536,2,64]{1,3,2,0:T(8,128)(2,1)} %bitcast.66, f32[64,12,1536]{2,1,0:T(8,128)S(1)} %get-tuple-element.45, f32[64,12]{1,0:T(8,128)S(1)} %max.37, pred[64,1536]{1,0:T(8,128)(4,1)S(1)} %copy-done.2), kind=kOutput, calls=%fused_computation.6 | convolution fusion | flops 910688256 | bytes 17599488 | tf_op jit(solution)/shard_map/rqp,rpd->rqd/dot_general | solution.py:195
  109.8 2.2 fusion.3
  112.2 1.4 convolution_add_fusion
  115.5 4.4 %collective-permute-done = f32[64,792]{1,0:T(8,128)S(1)} collective-permute-done((f32[64,792]{1,0:T(8,128)S(1)}, f32[64,792]{1,0:T(8,128)S(1)}, u32[]{:S(2)}, u32[]{:S(2)}) %collective-permute-start) | collective-permute-done | bytes 202784 | tf_op jit(solution)/shard_map/ppermute | solution.py:39
  122.6 2.3 multiply_add_fusion.2
  127.4 5.3 %collective-permute-done.1 = f32[64,792]{1,0:T(8,128)S(1)} collective-permute-done((f32[64,792]{1,0:T(8,128)S(1)}, f32[64,792]{1,0:T(8,128)S(1)}, u32[]{:S(2)}, u32[]{:S(2)}) %collective-permute-start.1) | collective-permute-done | bytes 202784 | tf_op jit(solution)/shard_map/ppermute | solution.py:39
  135.3 2.3 multiply_add_fusion.1
  139.3 4.6 %collective-permute-done.2 = f32[64,792]{1,0:T(8,128)S(1)} collective-permute-done((f32[64,792]{1,0:T(8,128)S(1)}, f32[64,792]{1,0:T(8,128)S(1)}, u32[]{:S(2)}, u32[]{:S(2)}) %collective-permute-start.2) | collective-permute-done | bytes 202784 | tf_op jit(solution)/shard_map/ppermute | solution.py:39
  146.6 2.3 multiply_add_fusion
  153.5 2.7 reshape.313
  156.2 2.5 copy.79
  158.7 2.6 reshape.314
  164.2 1.7 divide_convert_fusion
  166.2 2.6 fusion.61
  169.6 1.4 scatter_custom_fusion
  171.6 64.0 %all-reduce.3.cloned.1.call-done = f32[256,1536]{1,0:T(8,128)} async-done(((f32[256,1536]{1,0:T(8,128)}), f32[256,1536]{1,0:T(8,128)}) %all-reduce.3.cloned.1.call-update) | async-done | bytes 1572880 | tf_op jit(solution)/shard_map/psum | solution.py:209
  235.7 1.7 multiply_reduce_fusion
  240.1 2.1 convolution_bitcast_fusion
  243.0 4.6 %gather_fusion.2 = f32[512]{0:T(512)S(1)} fusion(f32[256,16]{0,1:T(8,128)S(1)} %fusion.62, s32[512]{0:T(512)S(1)} %reshape.337), kind=kCustom, calls=%fused_computation.2 | custom fusion | bytes 8192 | tf_op jit(solution)/shard_map/jit(take_along_axis)/gather | solution.py:213
  249.4 18.3 %all-reduce.5.cloned.1.call-done = f32[1,64,2,256]{3,1,2,0:T(8,128)} async-done(((f32[1,64,2,256]{3,1,2,0:T(8,128)}), f32[1,64,2,256]{3,1,2,0:T(8,128)}) %all-reduce.5.cloned.1.call-update) | async-done | bytes 131088 | tf_op jit(solution)/shard_map/psum | solution.py:238
  270.1 2.9 collective-permute-start.4
  273.0 9.1 %collective-permute-done.4 = f32[128,768]{1,0:T(8,128)S(1)} collective-permute-done((f32[128,768]{1,0:T(8,128)S(1)}, f32[128,768]{1,0:T(8,128)S(1)}, u32[]{:S(2)}, u32[]{:S(2)}) %collective-permute-start.4) | collective-permute-done | bytes 393248 | tf_op jit(solution)/shard_map/ppermute | solution.py:55
  282.2 1.4 collective-permute-start.5
  283.6 4.0 %collective-permute-done.5 = f32[64,768]{1,0:T(8,128)S(1)} collective-permute-done((f32[64,768]{1,0:T(8,128)S(1)}, f32[64,768]{1,0:T(8,128)S(1)}, u32[]{:S(2)}, u32[]{:S(2)}) %collective-permute-start.5) | collective-permute-done | bytes 196640 | tf_op jit(solution)/shard_map/ppermute | solution.py:55
  287.6 3.1 collective-permute-start.6
  290.7 2.0 collective-permute-done.6
  292.7 1.4 collective-permute-start.7
  294.2 1.8 collective-permute-done.7
  296.0 2.8 collective-permute-start.8
  298.8 1.5 collective-permute-done.8
  303.9 8.4 %psum.23 = f32[4]{0:T(128)S(1)} all-reduce(f32[4]{0:T(128)S(1)} %get-tuple-element.14), channel_id=1, replica_groups=mesh['seq'=16,'row'=2,'col'=4] {'row'}, use_global_device_ids=true, to_apply=%region_16.17 | all-reduce | flops 4 | bytes 32 | tf_op jit(solution)/shard_map/psum | solution.py:91
  315.5 2.9 collective-permute-start.11
  319.6 1.5 collective-permute-start.12
  322.3 3.1 collective-permute-start.13
  325.5 1.5 collective-permute-done.13
  327.0 1.3 collective-permute-start.14
  328.3 2.6 collective-permute-done.14
  330.9 2.8 collective-permute-start.15
  333.7 3.7 collective-permute-done.15
  337.3 1.6 fusion.11
  339.0 19.7 %reduce-scatter.2.cloned.1.call-done = f32[128,1024]{1,0:T(8,128)} async-done(((f32[256,1024]{1,0:T(8,128)}), f32[128,1024]{1,0:T(8,128)}) %reduce-scatter.2.cloned.1.call-update) | async-done | bytes 524304 | tf_op jit(solution)/shard_map/reduce_scatter | solution.py:257
  359.9 1.3 exponential_reduce_fusion
  361.2 1.4 collective-permute-start.16
  363.8 2.9 collective-permute-start.17
  367.8 1.5 collective-permute-start.18
  370.4 3.0 collective-permute-start.19
  374.4 1.4 collective-permute-start.20
  376.9 2.9 collective-permute-start.21
  381.0 8.6 %all-gather.1 = f32[1,256]{1,0:T(1,128)S(1)} all-gather(f32[1,128]{1,0:T(1,128)S(1)} %fusion.38), channel_id=3, replica_groups=mesh['seq'=16,'row'=2,'col'=4] {'row'}, dimensions={1}, use_global_device_ids=true | all-gather | bytes 1536 | tf_op jit(solution)/shard_map/all_gather | solution.py:279
  (157 shorter events, 56.5 us)
Async XLA Ops:
  7.2 330.2 %copy-start = (bf16[768,1024]{1,0:T(8,128)(2,1)S(1)}, bf16[768,1024]{1,0:T(8,128)(2,1)}, u32[]{:S(2)}) copy-start(bf16[768,1024]{1,0:T(8,128)(2,1)} %param.28) | copy-start | bytes 4718596
  7.2 52.0 %all-gather.4.cloned.1.call-start = ((), (), s32[]{:S(2)}) async-start(), calls=%async_computation.4 | async-start | bytes 2506752 | tf_op jit(solution)/shard_map/all_gather | solution.py:138
  11.5 224.1 %all-reduce.3.cloned.1.call-start = ((), (), s32[]{:S(2)}) async-start(), calls=%async_computation.1 | async-start | bytes 3145728 | tf_op jit(solution)/shard_map/psum | solution.py:209
  12.9 31.0 %copy-start.10 = (s32[64]{0:T(128)S(1)}, s32[64]{0:T(128)}, u32[]{:S(2)}) copy-start(s32[64]{0:T(128)} %param.21) | copy-start | bytes 772
  69.4 12.8 %slice-start = ((bf16[16,73728]{1,0:T(8,128)(2,1)}), bf16[16,12288]{1,0:T(8,128)(2,1)S(1)}, s32[]{:S(2)}) async-start(bf16[16,73728]{1,0:T(8,128)(2,1)} %reshape.359), calls=%async_computation.5 | async-start | bytes 786432 | tf_op jit(solution)/shard_map/slice | solution.py:142
  86.7 10.1 %copy-start.2 = (pred[64,1536]{1,0:T(8,128)(4,1)S(1)}, pred[64,1536]{1,0:T(8,128)(4,1)}, u32[]{:S(2)}) copy-start(pred[64,1536]{1,0:T(8,128)(4,1)} %broadcast_compare_fusion) | copy-start | bytes 294916
  109.8 17.5 %copy-start.8 = (s32[256,2]{0,1:T(2,128)S(1)}, s32[256,2]{0,1:T(2,128)}, u32[]{:S(2)}) copy-start(s32[256,2]{0,1:T(2,128)} %param.24) | copy-start | bytes 6148
  114.9 5.0 %collective-permute-start = (f32[64,792]{1,0:T(8,128)S(1)}, f32[64,792]{1,0:T(8,128)S(1)}, u32[]{:S(2)}, u32[]{:S(2)}) collective-permute-start(f32[64,792]{1,0:T(8,128)S(1)} %pad_maximum_fusion), channel_id=1, source_target_pairs={{0,8},{8,0},{16,24},{24,16},{32,40},{40,32},{48,56},{56,48},{64,72... | collective-permute-start | bytes 608264 | tf_op jit(solution)/shard_map/ppermute | solution.py:39
  119.9 0.7 copy-start.6
  126.2 6.5 %collective-permute-start.1 = (f32[64,792]{1,0:T(8,128)S(1)}, f32[64,792]{1,0:T(8,128)S(1)}, u32[]{:S(2)}, u32[]{:S(2)}) collective-permute-start(f32[64,792]{1,0:T(8,128)S(1)} %pad_maximum_fusion.1), channel_id=1, source_target_pairs={{0,16},{8,24},{16,0},{24,8},{32,48},{40,56},{48,32},{56,40},{64,80... | collective-permute-start | bytes 608264 | tf_op jit(solution)/shard_map/ppermute | solution.py:39
  132.7 0.7 copy-start.4
  139.0 5.0 %collective-permute-start.2 = (f32[64,792]{1,0:T(8,128)S(1)}, f32[64,792]{1,0:T(8,128)S(1)}, u32[]{:S(2)}, u32[]{:S(2)}) collective-permute-start(f32[64,792]{1,0:T(8,128)S(1)} %pad_maximum_fusion.2), channel_id=1, source_target_pairs={{0,32},{8,40},{16,48},{24,56},{32,0},{40,8},{48,16},{56,24},{64,96... | collective-permute-start | bytes 608264 | tf_op jit(solution)/shard_map/ppermute | solution.py:39
  143.9 0.7 copy-start.5
  150.9 10.4 %collective-permute-start.3 = (f32[64,792]{1,0:T(8,128)}, f32[64,792]{1,0:T(8,128)}, u32[]{:S(2)}, u32[]{:S(2)}) collective-permute-start(f32[64,792]{1,0:T(8,128)} %pad_maximum_fusion.3), channel_id=1, source_target_pairs={{0,64},{8,72},{16,80},{24,88},{32,96},{40,104},{48,112},{56,120},{... | collective-permute-start | bytes 608264 | tf_op jit(solution)/shard_map/ppermute | solution.py:39
  168.7 73.5 %copy-start.7 = (f32[1536,16]{0,1:T(8,128)S(1)}, f32[1536,16]{0,1:T(8,128)}, u32[]{:S(2)}) copy-start(f32[1536,16]{0,1:T(8,128)} %param.23) | copy-start | bytes 294916
  168.8 98.9 %all-reduce.5.cloned.1.call-start = ((), (), s32[]{:S(2)}) async-start(), calls=%async_computation.2 | async-start | bytes 262144 | tf_op jit(solution)/shard_map/psum | solution.py:238
  237.3 1.2 copy-start.1
  242.2 116.6 %reduce-scatter.2.cloned.1.call-start = ((), (), s32[]{:S(2)}) async-start(), calls=%async_computation.3 | async-start | bytes 1572864 | tf_op jit(solution)/shard_map/reduce_scatter | solution.py:257
  243.0 24.8 %copy-start.3 = (bf16[1,256,768]{2,1,0:T(8,128)(2,1)S(1)}, bf16[1,256,768]{2,1,0:T(8,128)(2,1)}, u32[]{:S(2)}) copy-start(bf16[1,256,768]{2,1,0:T(8,128)(2,1)} %param.26) | copy-start | bytes 1179652
  247.5 54.0 %copy-start.9 = (f32[1536]{0:T(1024)S(1)}, f32[1536]{0:T(1024)}, u32[]{:S(2)}) copy-start(f32[1536]{0:T(1024)} %param.27) | copy-start | bytes 18436
  248.7 90.2 %copy-start.11 = (s32[256]{0:T(256)S(1)}, s32[256]{0:T(256)}, u32[]{:S(2)}) copy-start(s32[256]{0:T(256)} %param.29) | copy-start | bytes 3076
  270.1 12.0 %collective-permute-start.4 = (f32[128,768]{1,0:T(8,128)S(1)}, f32[128,768]{1,0:T(8,128)S(1)}, u32[]{:S(2)}, u32[]{:S(2)}) collective-permute-start(f32[128,768]{1,0:T(8,128)S(1)} %slice_select_fusion), channel_id=1, source_target_pairs={{0,64},{1,65},{2,66},{3,67},{8,72},{9,73},{10,74},{11,75},{16,80},... | collective-permute-start | bytes 1179656 | tf_op jit(solution)/shard_map/ppermute | solution.py:55
  282.2 5.4 %collective-permute-start.5 = (f32[64,768]{1,0:T(8,128)S(1)}, f32[64,768]{1,0:T(8,128)S(1)}, u32[]{:S(2)}, u32[]{:S(2)}) collective-permute-start(f32[64,768]{1,0:T(8,128)S(1)} %slice_select_fusion.1), channel_id=1, source_target_pairs={{0,32},{1,33},{2,34},{3,35},{8,40},{9,41},{10,42},{11,43},{16,48},... | collective-permute-start | bytes 589832 | tf_op jit(solution)/shard_map/ppermute | solution.py:55
  287.6 5.1 %collective-permute-start.6 = (f32[32,768]{1,0:T(8,128)S(1)}, f32[32,768]{1,0:T(8,128)S(1)}, u32[]{:S(2)}, u32[]{:S(2)}) collective-permute-start(f32[32,768]{1,0:T(8,128)S(1)} %slice_select_fusion.2), channel_id=1, source_target_pairs={{0,16},{1,17},{2,18},{3,19},{8,24},{9,25},{10,26},{11,27},{16,0},{... | collective-permute-start | bytes 294920 | tf_op jit(solution)/shard_map/ppermute | solution.py:55
  292.7 3.3 collective-permute-start.7
  296.0 4.3 %collective-permute-start.8 = (f32[8,768]{1,0:T(8,128)S(1)}, f32[8,768]{1,0:T(8,128)S(1)}, u32[]{:S(2)}, u32[]{:S(2)}) collective-permute-start(f32[8,768]{1,0:T(8,128)S(1)} %slice_select_fusion.4), channel_id=1, source_target_pairs={{0,2},{1,3},{2,0},{3,1},{8,10},{9,11},{10,8},{11,9},{16,18},{17,19... | collective-permute-start | bytes 73736 | tf_op jit(solution)/shard_map/ppermute | solution.py:55
  300.3 2.6 collective-permute-start.9
  313.0 2.5 collective-permute-start.10
  315.5 4.1 %collective-permute-start.11 = (bf16[8,768]{1,0:T(8,128)(2,1)S(1)}, bf16[8,768]{1,0:T(8,128)(2,1)S(1)}, u32[]{:S(2)}, u32[]{:S(2)}) collective-permute-start(bf16[8,768]{1,0:T(8,128)(2,1)S(1)} %maximum_select_fusion.6), channel_id=1, source_target_pairs={{0,2},{1,3},{2,0},{3,1},{8,10},{9,11},{10,8},{11,9},{16,18},{17,19... | collective-permute-start | bytes 36872 | tf_op jit(solution)/shard_map/ppermute | solution.py:66
  319.6 2.7 collective-permute-start.12
  322.3 4.6 %collective-permute-start.13 = (bf16[32,768]{1,0:T(8,128)(2,1)S(1)}, bf16[32,768]{1,0:T(8,128)(2,1)S(1)}, u32[]{:S(2)}, u32[]{:S(2)}) collective-permute-start(bf16[32,768]{1,0:T(8,128)(2,1)S(1)} %maximum_select_fusion.4), channel_id=1, source_target_pairs={{0,16},{1,17},{2,18},{3,19},{8,24},{9,25},{10,26},{11,27},{16,0},{... | collective-permute-start | bytes 147464 | tf_op jit(solution)/shard_map/ppermute | solution.py:66
  327.0 3.8 collective-permute-start.14
  330.9 6.5 %collective-permute-start.15 = (bf16[128,768]{1,0:T(8,128)(2,1)S(1)}, bf16[128,768]{1,0:T(8,128)(2,1)S(1)}, u32[]{:S(2)}, u32[]{:S(2)}) collective-permute-start(bf16[128,768]{1,0:T(8,128)(2,1)S(1)} %maximum_select_fusion.2), channel_id=1, source_target_pairs={{0,64},{1,65},{2,66},{3,67},{8,72},{9,73},{10,74},{11,75},{16,80},... | collective-permute-start | bytes 589832 | tf_op jit(solution)/shard_map/ppermute | solution.py:66
  361.2 2.5 collective-permute-start.16
  363.8 4.0 %collective-permute-start.17 = (f32[1,384]{1,0:T(1,128)S(1)}, f32[1,384]{1,0:T(1,128)S(1)}, u32[]{:S(2)}, u32[]{:S(2)}) collective-permute-start(f32[1,384]{1,0:T(1,128)S(1)} %pad_maximum_fusion.6), channel_id=1, source_target_pairs={{0,2},{1,3},{2,0},{3,1},{8,10},{9,11},{10,8},{11,9},{16,18},{17,19... | collective-permute-start | bytes 4616 | tf_op jit(solution)/shard_map/ppermute | solution.py:39
  367.8 2.5 collective-permute-start.18
  370.4 4.0 %collective-permute-start.19 = (f32[1,384]{1,0:T(1,128)S(1)}, f32[1,384]{1,0:T(1,128)S(1)}, u32[]{:S(2)}, u32[]{:S(2)}) collective-permute-start(f32[1,384]{1,0:T(1,128)S(1)} %pad_maximum_fusion.8), channel_id=1, source_target_pairs={{0,16},{1,17},{2,18},{3,19},{8,24},{9,25},{10,26},{11,27},{16,0},{... | collective-permute-start | bytes 4616 | tf_op jit(solution)/shard_map/ppermute | solution.py:39
  374.4 2.5 collective-permute-start.20
  376.9 4.0 %collective-permute-start.21 = (f32[1,384]{1,0:T(1,128)S(1)}, f32[1,384]{1,0:T(1,128)S(1)}, u32[]{:S(2)}, u32[]{:S(2)}) collective-permute-start(f32[1,384]{1,0:T(1,128)S(1)} %pad_maximum_fusion.10), channel_id=1, source_target_pairs={{0,64},{1,65},{2,66},{3,67},{8,72},{9,73},{10,74},{11,75},{16,80},... | collective-permute-start | bytes 4616 | tf_op jit(solution)/shard_map/ppermute | solution.py:39
Sparse Core Ops, SparseCore 0:
  11.6 47.4 all-gather.3
  168.9 66.7 all-reduce.2
  242.3 25.3 all-reduce.4
  339.1 19.6 reduce-scatter.1
where the time goes:
time: 399 us; the launch traced here: 397 us
  waiting for transfers between devices  169 us (42%)
  local copies, waits for them, and re-layouts  82.7 us (21%)
  starting transfers between devices  42 us (11%)
  matrix products  38.1 us (10%)
  other arithmetic  33.8 us (8%)
  blocking collectives  17.1 us (4%)
  between operations  14.3 us (4%)
    psum x1, waiting for transfers between devices, on_device(): state_mid = state_in + lax.psum(partial_out, ('row', 'col'))  64 us
    unnamed x27, local copies, waits for them, and re-layouts  35.7 us
    ppermute x10, waiting for transfers between devices, butterfly_merge(): other = lax.ppermute(packed, axes, pairs)  20.9 us
    reduce_scatter x1, waiting for transfers between devices, on_device(): lax.psum_scatter(jnp.dot(normed_out, w_head, preferred_element_type=jnp.f...  19.7 us
    ppermute x6, waiting for transfers between devices, halving_scatter(): value = keep + lax.ppermute(send, axes, pairs)  19.7 us
    psum x1, waiting for transfers between devices, on_device(): gate_both = lax.psum(gate_part, 'row')  18.3 us
    ppermute x10, starting transfers between devices, butterfly_merge(): other = lax.ppermute(packed, axes, pairs)  16.2 us
    all_gather x1, waiting for transfers between devices, on_device(): packed = lax.all_gather(jnp.concatenate(pieces), 'seq', axis=0, tiled=False)  14.5 us
  transfers between devices with their start and end apart: 26, of which 25 were waited for; matrix products, arithmetic and copies ran while one was open for 13% of the time, Pallas kernels for 0%

commit v1 on v0

--- a/solution.py
+++ b/solution.py
@@ -39,6 +39,31 @@
         other = lax.ppermute(packed, axes, pairs)
         packed = jnp.concatenate(combine(split(packed), split(other)), axis=-1)
         step *= 2
+    return split(packed)
+
+
+def halving_merge(value, axes, count, combine):
+    widths = [part.shape[-1] for part in value]
+    edges = [0]
+    for width in widths:
+        edges.append(edges[-1] + width)
+
+    def split(packed):
+        return tuple(packed[..., edges[i] : edges[i + 1]] for i in range(len(widths)))
+
+    index = lax.axis_index(axes)
+    packed = jnp.concatenate(value, axis=-1)
+    step = count // 2
+    while step >= 1:
+        half = packed.shape[0] // 2
+        upper = (index // step) % 2 == 1
+        low, high = packed[:half], packed[half:]
+        send = jnp.where(upper, low, high)
+        keep = jnp.where(upper, high, low)
+        pairs = [(i, i ^ step) for i in range(count)]
+        other = lax.ppermute(send, axes, pairs)
+        packed = jnp.concatenate(combine(split(keep), split(other)), axis=-1)
+        step //= 2
     return split(packed)
 
 
@@ -196,19 +221,20 @@
     mixed = mixed + jnp.einsum(
         "rqu,rud->rqd", new_weights, fresh_values, precision=lax.Precision.HIGHEST
     )
-    highest, totals, mixed = butterfly_merge(
+    highest, totals, mixed = halving_merge(
         (highest, totals, mixed.reshape(requests, -1)), "seq", seq_count, merge_softmax
     )
-    attended = mixed.reshape(requests, NEW * group, HD) / totals[..., None]
-    attn_mix = attended.reshape(total_rows, query_cols).astype(jnp.bfloat16)
+    own_requests = requests // seq_count
+    attended = mixed.reshape(own_requests, NEW * group, HD) / totals[..., None]
+    attn_mix = attended.reshape(own_count, query_cols).astype(jnp.bfloat16)
     partial_out = jnp.dot(
         attn_mix,
         w_out_all,
         preferred_element_type=jnp.float32,
     )
-    state_mid = state_in + lax.psum(partial_out, ("row", "col"))
-    own_mid = lax.dynamic_slice_in_dim(state_mid, block_start, own_count, 0)
-    normed_mid = rms_scale(state_mid, ffn_gain).astype(jnp.bfloat16)
+    own_mid = hidden_in.astype(jnp.float32) + lax.psum(partial_out, ("row", "col"))
+    own_normed = rms_scale(own_mid, ffn_gain).astype(jnp.bfloat16)
+    normed_mid = doubling_gather(own_normed, "seq", seq_count)
     router = jnp.dot(normed_mid.astype(jnp.float32), w_router, precision=lax.Precision.HIGHEST)
     chosen = jnp.take_along_axis(router, routes, axis=1)
     probs = jax.nn.sigmoid(chosen - chosen[:, ::-1])
@@ -245,7 +271,7 @@
     block_count = seq_count * lax.axis_size("col")
     out_count = total_rows // block_count
     block_mid = lax.dynamic_slice_in_dim(
-        lax.dynamic_slice_in_dim(state_mid, block_index * out_count, out_count, 0), col_start, half, 1
+        lax.dynamic_slice_in_dim(own_mid, col_index * out_count, out_count, 0), col_start, half, 1
     )
     state_out = halving_scatter(term, ("seq", "col"), block_count) + block_mid
     layer_out = state_out.astype(jnp.bfloat16)

time: 399 us -> 375 us (0.940)
  local copies, waits for them, and re-layouts: 82.7 us -> 64 us
  other arithmetic: 33.8 us -> 18.4 us
  starting transfers between devices: 42 us -> 50.3 us
  waiting for transfers between devices: 169 us -> 177 us
  matrix products: 38.1 us -> 32.1 us
    ppermute x10 -> x6, waiting for transfers between devices: 20.9 us -> 6.53 us  [butterfly_merge(): other = lax.ppermute(packed, axes, pairs)]
    ppermute x6 -> x10, waiting for transfers between devices: 11.4 us -> 23.6 us  [doubling_gather(): other = lax.ppermute(value, axes, pairs)]
    ppermute x0 -> x4, waiting for transfers between devices: none -> 10.3 us  [halving_merge(): other = lax.ppermute(send, axes, pairs)]
    ppermute x6 -> x10, starting transfers between devices: 12.9 us -> 21.2 us  [doubling_gather(): other = lax.ppermute(value, axes, pairs)]
    add x3, other arithmetic: 6.99 us -> 0.29 us  [merge_softmax(): shaped_a + shaped_b]
    convert_element_type x3 -> x2, other arithmetic: 4.95 us -> 0.19 us  [the longest x1 0.11 us: on_device(): attn_mix = attended.reshape(own_count, query_cols).astype(jnp.bfloat16)]
    ppermute x10 -> x6, starting transfers between devices: 16.2 us -> 13 us  [butterfly_merge(): other = lax.ppermute(packed, axes, pairs)]
    unnamed x27 -> x23, local copies, waits for them, and re-layouts: 35.7 us -> 34.1 us
  transfers between devices with their start and end apart: 26 -> 30, of which waited for: 25 -> 29; matrix products, arithmetic and copies ran while one was open for 13% -> 12% of each run, Pallas kernels for 0% -> 0%
where the time goes in v1:
time: 375 us; the launch traced here: 373 us
  waiting for transfers between devices  177 us (47%)
  local copies, waits for them, and re-layouts  64 us (17%)
  starting transfers between devices  50.3 us (13%)
  matrix products  32.1 us (9%)
  other arithmetic  18.4 us (5%)
  blocking collectives  17 us (5%)
  between operations  14.5 us (4%)
    psum x1, waiting for transfers between devices, on_device(): lax.psum(partial_out, ('row', 'col'))  60.7 us
    unnamed x23, local copies, waits for them, and re-layouts  34.1 us
    ppermute x10, waiting for transfers between devices, doubling_gather(): other = lax.ppermute(value, axes, pairs)  23.6 us
    psum x1, waiting for transfers between devices, on_device(): gate_both = lax.psum(gate_part, 'row')  22.1 us
    ppermute x10, starting transfers between devices, doubling_gather(): other = lax.ppermute(value, axes, pairs)  21.2 us
    reduce_scatter x1, waiting for transfers between devices, on_device(): lax.psum_scatter(jnp.dot(normed_out, w_head, preferred_element_type=jnp.f...  19.8 us
    ppermute x6, waiting for transfers between devices, halving_scatter(): value = keep + lax.ppermute(send, axes, pairs)  19.8 us
    all_gather x1, waiting for transfers between devices, on_device(): packed = lax.all_gather(jnp.concatenate(pieces), 'seq', axis=0, tiled=False)  14.1 us
  transfers between devices with their start and end apart: 30, of which 29 were waited for; matrix products, arithmetic and copies ran while one was open for 12% of the time, Pallas kernels for 0%

profile of v1, /device:TPU:1, one launch (start us, length us, event | category | flops | bytes accessed | tf_op | source)
XLA Modules:
  0.0 373.3 jit_solution(4170985505013345955)
XLA Ops:
  10.1 1.4 pad_maximum_fusion.1
  12.3 32.6 %copy.74 = bf16[64,1536,128]{1,2,0:T(8,128)(2,1)} copy(bf16[64,1536,128]{2,1,0:T(8,128)(2,1)} %param.20) | data formatting | bytes 50331648 | tf_op args[5]
  45.1 14.1 %all-gather.4.cloned.1.call-done = bf16[1179648]{0:T(1024)(128)(2,1)} async-done(((bf16[73728]{0:T(1024)(128)(2,1)}), bf16[1179648]{0:T(1024)(128)(2,1)}) %all-gather.4.cloned.1.call-update) | async-done | bytes 2359312 | tf_op jit(solution)/shard_map/all_gather | solution.py:163
  59.2 3.3 reshape.384
  63.7 2.4 fusion.62
  66.1 1.4 mul.287
  67.5 1.6 reduce_sum.81
  70.3 2.3 fusion.10
  72.6 1.5 convert_element_type.69
  74.1 2.9 reshape.331
  76.9 2.2 fusion.65
  81.2 1.3 convolution_convert_fusion
  83.4 8.2 %fusion.2 = (f32[64,12]{1,0:T(8,128)S(1)}, f32[64,12,1536]{2,1,0:T(8,128)S(1)}) fusion(pred[64,1536]{1,0:T(8,128)(4,1)S(1)} %broadcast_compare_fusion, f32[64,12,64]{2,1,0:T(8,128)S(1)} %reshape.332, bf16[64,1536,2,64]{1,3,2,0:T(8,128)(2,1)} %bitcast.65), kind=kOutput, calls=%fused_computation.11 | convolution fusion | flops 909507840 | bytes 17599488 | tf_op jit(solution)/shard_map/rqd,rpd->rqp/dot_general | solution.py:201
  91.6 12.9 %fusion = f32[64,12,64]{2,1,0:T(8,128)S(1)} fusion(bf16[64,1536,2,64]{1,3,2,0:T(8,128)(2,1)} %bitcast.66, f32[64,12,1536]{2,1,0:T(8,128)S(1)} %get-tuple-element.53, f32[64,12]{1,0:T(8,128)S(1)} %max.37, pred[64,1536]{1,0:T(8,128)(4,1)S(1)} %broadcast_compare_fusion), kind=kOutput, calls=%fused_computation.6 | convolution fusion | flops 910688256 | bytes 17599488 | tf_op jit(solution)/shard_map/rqp,rpd->rqd/dot_general | solution.py:220
  104.6 2.4 fusion.3
  108.1 1.3 collective-permute-start
  109.4 4.0 %collective-permute-done = f32[32,792]{1,0:T(8,128)S(1)} collective-permute-done((f32[32,792]{1,0:T(8,128)S(1)}, f32[32,792]{1,0:T(8,128)S(1)}, u32[]{:S(2)}, u32[]{:S(2)}) %collective-permute-start) | collective-permute-done | bytes 101408 | tf_op jit(solution)/shard_map/ppermute | solution.py:64
  114.4 2.8 collective-permute-done.1
  118.7 3.6 collective-permute-done.2
  127.5 60.7 %all-reduce.3.cloned.1.call-done = f32[16,1536]{1,0:T(8,128)} async-done(((f32[16,1536]{1,0:T(8,128)}), f32[16,1536]{1,0:T(8,128)}) %all-reduce.3.cloned.1.call-update) | async-done | bytes 98320 | tf_op jit(solution)/shard_map/psum | solution.py:235
  189.3 1.4 collective-permute-start.4
  190.8 1.6 collective-permute-done.4
  192.4 3.0 collective-permute-start.5
  195.7 1.9 collective-permute-done.5
  197.6 1.3 collective-permute-start.6
  198.9 1.4 scatter_custom_fusion
  200.4 1.9 collective-permute-done.6
  202.3 2.8 collective-permute-start.7
  205.8 6.9 %collective-permute-done.7 = bf16[128,1536]{1,0:T(8,128)(2,1)S(1)} collective-permute-done((bf16[128,1536]{1,0:T(8,128)(2,1)S(1)}, bf16[128,1536]{1,0:T(8,128)(2,1)S(1)}, u32[]{:S(2)}, u32[]{:S(2)}) %collective-permute-start.7) | collective-permute-done | bytes 393248 | tf_op jit(solution)/shard_map/ppermute | solution.py:91
  213.6 2.0 convolution_bitcast_fusion
  216.4 4.6 %gather_fusion.2 = f32[512]{0:T(512)S(1)} fusion(f32[256,16]{0,1:T(8,128)S(1)} %fusion.67, s32[512]{0:T(512)S(1)} %reshape.362), kind=kCustom, calls=%fused_computation.2 | custom fusion | bytes 8192 | tf_op jit(solution)/shard_map/jit(take_along_axis)/gather | solution.py:239
  222.8 22.1 %all-reduce.5.cloned.1.call-done = f32[1,64,2,256]{3,1,2,0:T(8,128)} async-done(((f32[1,64,2,256]{3,1,2,0:T(8,128)}), f32[1,64,2,256]{3,1,2,0:T(8,128)}) %all-reduce.5.cloned.1.call-update) | async-done | bytes 131088 | tf_op jit(solution)/shard_map/psum | solution.py:264
  247.2 3.1 collective-permute-start.8
  250.3 9.1 %collective-permute-done.8 = f32[128,768]{1,0:T(8,128)S(1)} collective-permute-done((f32[128,768]{1,0:T(8,128)S(1)}, f32[128,768]{1,0:T(8,128)S(1)}, u32[]{:S(2)}, u32[]{:S(2)}) %collective-permute-start.8) | collective-permute-done | bytes 393248 | tf_op jit(solution)/shard_map/ppermute | solution.py:80
  259.5 1.4 collective-permute-start.9
  260.9 4.1 %collective-permute-done.9 = f32[64,768]{1,0:T(8,128)S(1)} collective-permute-done((f32[64,768]{1,0:T(8,128)S(1)}, f32[64,768]{1,0:T(8,128)S(1)}, u32[]{:S(2)}, u32[]{:S(2)}) %collective-permute-start.9) | collective-permute-done | bytes 196640 | tf_op jit(solution)/shard_map/ppermute | solution.py:80
  265.0 3.1 collective-permute-start.10
  268.1 2.0 collective-permute-done.10
  270.1 1.4 collective-permute-start.11
  271.6 1.9 collective-permute-done.11
  273.4 2.8 collective-permute-start.12
  276.2 1.5 collective-permute-done.12
  277.7 1.3 collective-permute-start.13
  279.1 1.3 collective-permute-done.13
  280.5 8.4 %psum.23 = f32[4]{0:T(128)S(1)} all-reduce(f32[4]{0:T(128)S(1)} %get-tuple-element.14), channel_id=1, replica_groups=mesh['seq'=16,'row'=2,'col'=4] {'row'}, use_global_device_ids=true, to_apply=%region_16.17 | all-reduce | flops 4 | bytes 32 | tf_op jit(solution)/shard_map/psum | solution.py:116
  289.6 1.3 collective-permute-start.14
  292.1 2.9 collective-permute-start.15
  296.2 1.5 collective-permute-start.16
  298.9 3.1 collective-permute-start.17
  302.0 1.5 collective-permute-done.17
  303.6 1.3 collective-permute-start.18
  304.8 2.6 collective-permute-done.18
  307.4 2.8 collective-permute-start.19
  310.2 3.6 collective-permute-done.19
  313.9 1.5 fusion.13
  315.6 19.8 %reduce-scatter.2.cloned.1.call-done = f32[128,1024]{1,0:T(8,128)} async-done(((f32[256,1024]{1,0:T(8,128)}), f32[128,1024]{1,0:T(8,128)}) %reduce-scatter.2.cloned.1.call-update) | async-done | bytes 524304 | tf_op jit(solution)/shard_map/reduce_scatter | solution.py:283
  336.5 1.3 exponential_reduce_fusion
  337.8 1.4 collective-permute-start.20
  340.4 2.9 collective-permute-start.21
  344.4 1.4 collective-permute-start.22
  346.9 3.0 collective-permute-start.23
  351.0 1.4 collective-permute-start.24
  353.5 2.9 collective-permute-start.25
  357.6 8.6 %all-gather.1 = f32[1,256]{1,0:T(1,128)S(1)} all-gather(f32[1,128]{1,0:T(1,128)S(1)} %fusion.43), channel_id=3, replica_groups=mesh['seq'=16,'row'=2,'col'=4] {'row'}, dimensions={1}, use_global_device_ids=true | all-gather | bytes 1536 | tf_op jit(solution)/shard_map/all_gather | solution.py:305
  (174 shorter events, 39.2 us)
Async XLA Ops:
  7.2 306.7 %copy-start = (bf16[768,1024]{1,0:T(8,128)(2,1)S(1)}, bf16[768,1024]{1,0:T(8,128)(2,1)}, u32[]{:S(2)}) copy-start(bf16[768,1024]{1,0:T(8,128)(2,1)} %param.28) | copy-start | bytes 4718596
  7.2 52.0 %all-gather.4.cloned.1.call-start = ((), (), s32[]{:S(2)}) async-start(), calls=%async_computation.4 | async-start | bytes 2506752 | tf_op jit(solution)/shard_map/all_gather | solution.py:163
  11.5 176.7 %all-reduce.3.cloned.1.call-start = ((), (), s32[]{:S(2)}) async-start(), calls=%async_computation.1 | async-start | bytes 196608 | tf_op jit(solution)/shard_map/psum | solution.py:235
  12.3 32.6 %copy-start.8 = (s32[64]{0:T(128)S(1)}, s32[64]{0:T(128)}, u32[]{:S(2)}) copy-start(s32[64]{0:T(128)} %param.21) | copy-start | bytes 772
  69.4 10.8 %slice-start = ((bf16[16,73728]{1,0:T(8,128)(2,1)}), bf16[16,12288]{1,0:T(8,128)(2,1)S(1)}, s32[]{:S(2)}) async-start(bf16[16,73728]{1,0:T(8,128)(2,1)} %reshape.384), calls=%async_computation.5 | async-start | bytes 786432 | tf_op jit(solution)/shard_map/slice | solution.py:167
  104.5 14.1 %copy-start.5 = (s32[256,2]{0,1:T(2,128)S(1)}, s32[256,2]{0,1:T(2,128)}, u32[]{:S(2)}) copy-start(s32[256,2]{0,1:T(2,128)} %param.24) | copy-start | bytes 6148
  104.5 18.8 %copy-start.1 = (bf16[16,18432]{1,0:T(8,128)(2,1)S(1)}, bf16[16,18432]{1,0:T(8,128)(2,1)}, u32[]{:S(2)}) copy-start(bf16[16,18432]{1,0:T(8,128)(2,1)} %get-tuple-element.33) | copy-start | bytes 1769476
  107.1 81.1 %copy-start.3 = (bf16[16,1536]{1,0:T(8,128)(2,1)S(1)}, bf16[16,1536]{1,0:T(8,128)(2,1)}, u32[]{:S(2)}) copy-start(bf16[16,1536]{1,0:T(8,128)(2,1)} %param.15) | copy-start | bytes 147460
  107.1 82.1 %copy-start.6 = (f32[1536]{0:T(1024)S(1)}, f32[1536]{0:T(1024)}, u32[]{:S(2)}) copy-start(f32[1536]{0:T(1024)} %param.22) | copy-start | bytes 18436
  108.1 5.2 %collective-permute-start = (f32[32,792]{1,0:T(8,128)S(1)}, f32[32,792]{1,0:T(8,128)S(1)}, u32[]{:S(2)}, u32[]{:S(2)}) collective-permute-start(f32[32,792]{1,0:T(8,128)S(1)} %get-tuple-element.36), channel_id=1, source_target_pairs={{0,64},{8,72},{16,80},{24,88},{32,96},{40,104},{48,112},{56,120},{... | collective-permute-start | bytes 304136 | tf_op jit(solution)/shard_map/ppermute | solution.py:64
  114.1 3.1 collective-permute-start.1
  117.9 97.8 %copy-start.4 = (f32[1536,16]{0,1:T(8,128)S(1)}, f32[1536,16]{0,1:T(8,128)}, u32[]{:S(2)}) copy-start(f32[1536,16]{0,1:T(8,128)} %param.23) | copy-start | bytes 294916
  117.9 4.3 %collective-permute-start.2 = (f32[8,792]{1,0:T(8,128)S(1)}, f32[8,792]{1,0:T(8,128)S(1)}, u32[]{:S(2)}, u32[]{:S(2)}) collective-permute-start(f32[8,792]{1,0:T(8,128)S(1)} %get-tuple-element.42), channel_id=1, source_target_pairs={{0,16},{8,24},{16,0},{24,8},{32,48},{40,56},{48,32},{56,40},{64,80... | collective-permute-start | bytes 76040 | tf_op jit(solution)/shard_map/ppermute | solution.py:64
  122.8 2.9 collective-permute-start.3
  127.0 117.9 %all-reduce.5.cloned.1.call-start = ((), (), s32[]{:S(2)}) async-start(), calls=%async_computation.2 | async-start | bytes 262144 | tf_op jit(solution)/shard_map/psum | solution.py:264
  189.3 3.0 collective-permute-start.4
  192.4 5.2 %collective-permute-start.5 = (bf16[32,1536]{1,0:T(8,128)(2,1)S(1)}, bf16[32,1536]{1,0:T(8,128)(2,1)S(1)}, u32[]{:S(2)}, u32[]{:S(2)}) collective-permute-start(bf16[32,1536]{1,0:T(8,128)(2,1)S(1)} %maximum_select_fusion.6), channel_id=1, source_target_pairs={{0,16},{8,24},{16,0},{24,8},{32,48},{40,56},{48,32},{56,40},{64,80... | collective-permute-start | bytes 294920 | tf_op jit(solution)/shard_map/ppermute | solution.py:91
  197.6 4.6 %collective-permute-start.6 = (bf16[64,1536]{1,0:T(8,128)(2,1)S(1)}, bf16[64,1536]{1,0:T(8,128)(2,1)S(1)}, u32[]{:S(2)}, u32[]{:S(2)}) collective-permute-start(bf16[64,1536]{1,0:T(8,128)(2,1)S(1)} %maximum_select_fusion.4), channel_id=1, source_target_pairs={{0,32},{8,40},{16,48},{24,56},{32,0},{40,8},{48,16},{56,24},{64,96... | collective-permute-start | bytes 589832 | tf_op jit(solution)/shard_map/ppermute | solution.py:91
  202.3 10.3 %collective-permute-start.7 = (bf16[128,1536]{1,0:T(8,128)(2,1)S(1)}, bf16[128,1536]{1,0:T(8,128)(2,1)S(1)}, u32[]{:S(2)}, u32[]{:S(2)}) collective-permute-start(bf16[128,1536]{1,0:T(8,128)(2,1)S(1)} %maximum_select_fusion.1), channel_id=1, source_target_pairs={{0,64},{8,72},{16,80},{24,88},{32,96},{40,104},{48,112},{56,120},{... | collective-permute-start | bytes 1179656 | tf_op jit(solution)/shard_map/ppermute | solution.py:91
  215.6 119.7 %reduce-scatter.2.cloned.1.call-start = ((), (), s32[]{:S(2)}) async-start(), calls=%async_computation.3 | async-start | bytes 1572864 | tf_op jit(solution)/shard_map/reduce_scatter | solution.py:283
  216.4 28.5 %copy-start.2 = (bf16[1,256,768]{2,1,0:T(8,128)(2,1)S(1)}, bf16[1,256,768]{2,1,0:T(8,128)(2,1)}, u32[]{:S(2)}) copy-start(bf16[1,256,768]{2,1,0:T(8,128)(2,1)} %param.26) | copy-start | bytes 1179652
  221.0 58.0 %copy-start.7 = (f32[1536]{0:T(1024)S(1)}, f32[1536]{0:T(1024)}, u32[]{:S(2)}) copy-start(f32[1536]{0:T(1024)} %param.27) | copy-start | bytes 18436
  222.1 93.3 %copy-start.9 = (s32[256]{0:T(256)S(1)}, s32[256]{0:T(256)}, u32[]{:S(2)}) copy-start(s32[256]{0:T(256)} %param.29) | copy-start | bytes 3076
  247.2 12.2 %collective-permute-start.8 = (f32[128,768]{1,0:T(8,128)S(1)}, f32[128,768]{1,0:T(8,128)S(1)}, u32[]{:S(2)}, u32[]{:S(2)}) collective-permute-start(f32[128,768]{1,0:T(8,128)S(1)} %slice_select_fusion), channel_id=1, source_target_pairs={{0,64},{1,65},{2,66},{3,67},{8,72},{9,73},{10,74},{11,75},{16,80},... | collective-permute-start | bytes 1179656 | tf_op jit(solution)/shard_map/ppermute | solution.py:80
  259.5 5.4 %collective-permute-start.9 = (f32[64,768]{1,0:T(8,128)S(1)}, f32[64,768]{1,0:T(8,128)S(1)}, u32[]{:S(2)}, u32[]{:S(2)}) collective-permute-start(f32[64,768]{1,0:T(8,128)S(1)} %slice_select_fusion.1), channel_id=1, source_target_pairs={{0,32},{1,33},{2,34},{3,35},{8,40},{9,41},{10,42},{11,43},{16,48},... | collective-permute-start | bytes 589832 | tf_op jit(solution)/shard_map/ppermute | solution.py:80
  265.0 5.1 %collective-permute-start.10 = (f32[32,768]{1,0:T(8,128)S(1)}, f32[32,768]{1,0:T(8,128)S(1)}, u32[]{:S(2)}, u32[]{:S(2)}) collective-permute-start(f32[32,768]{1,0:T(8,128)S(1)} %slice_select_fusion.4), channel_id=1, source_target_pairs={{0,16},{1,17},{2,18},{3,19},{8,24},{9,25},{10,26},{11,27},{16,0},{... | collective-permute-start | bytes 294920 | tf_op jit(solution)/shard_map/ppermute | solution.py:80
  270.1 3.3 collective-permute-start.11
  273.4 4.3 %collective-permute-start.12 = (f32[8,768]{1,0:T(8,128)S(1)}, f32[8,768]{1,0:T(8,128)S(1)}, u32[]{:S(2)}, u32[]{:S(2)}) collective-permute-start(f32[8,768]{1,0:T(8,128)S(1)} %slice_select_fusion.10), channel_id=1, source_target_pairs={{0,2},{1,3},{2,0},{3,1},{8,10},{9,11},{10,8},{11,9},{16,18},{17,19... | collective-permute-start | bytes 73736 | tf_op jit(solution)/shard_map/ppermute | solution.py:80
  277.7 2.6 collective-permute-start.13
  289.6 2.5 collective-permute-start.14
  292.1 4.1 %collective-permute-start.15 = (bf16[8,768]{1,0:T(8,128)(2,1)S(1)}, bf16[8,768]{1,0:T(8,128)(2,1)S(1)}, u32[]{:S(2)}, u32[]{:S(2)}) collective-permute-start(bf16[8,768]{1,0:T(8,128)(2,1)S(1)} %maximum_select_fusion.10), channel_id=1, source_target_pairs={{0,2},{1,3},{2,0},{3,1},{8,10},{9,11},{10,8},{11,9},{16,18},{17,19... | collective-permute-start | bytes 36872 | tf_op jit(solution)/shard_map/ppermute | solution.py:91
  296.2 2.7 collective-permute-start.16
  298.9 4.6 %collective-permute-start.17 = (bf16[32,768]{1,0:T(8,128)(2,1)S(1)}, bf16[32,768]{1,0:T(8,128)(2,1)S(1)}, u32[]{:S(2)}, u32[]{:S(2)}) collective-permute-start(bf16[32,768]{1,0:T(8,128)(2,1)S(1)} %maximum_select_fusion.8), channel_id=1, source_target_pairs={{0,16},{1,17},{2,18},{3,19},{8,24},{9,25},{10,26},{11,27},{16,0},{... | collective-permute-start | bytes 147464 | tf_op jit(solution)/shard_map/ppermute | solution.py:91
  303.6 3.8 %collective-permute-start.18 = (bf16[64,768]{1,0:T(8,128)(2,1)S(1)}, bf16[64,768]{1,0:T(8,128)(2,1)S(1)}, u32[]{:S(2)}, u32[]{:S(2)}) collective-permute-start(bf16[64,768]{1,0:T(8,128)(2,1)S(1)} %maximum_select_fusion.7), channel_id=1, source_target_pairs={{0,32},{1,33},{2,34},{3,35},{8,40},{9,41},{10,42},{11,43},{16,48},... | collective-permute-start | bytes 294920 | tf_op jit(solution)/shard_map/ppermute | solution.py:91
  307.4 6.5 %collective-permute-start.19 = (bf16[128,768]{1,0:T(8,128)(2,1)S(1)}, bf16[128,768]{1,0:T(8,128)(2,1)S(1)}, u32[]{:S(2)}, u32[]{:S(2)}) collective-permute-start(bf16[128,768]{1,0:T(8,128)(2,1)S(1)} %maximum_select_fusion.5), channel_id=1, source_target_pairs={{0,64},{1,65},{2,66},{3,67},{8,72},{9,73},{10,74},{11,75},{16,80},... | collective-permute-start | bytes 589832 | tf_op jit(solution)/shard_map/ppermute | solution.py:91
  337.8 2.5 collective-permute-start.20
  340.4 4.0 %collective-permute-start.21 = (f32[1,384]{1,0:T(1,128)S(1)}, f32[1,384]{1,0:T(1,128)S(1)}, u32[]{:S(2)}, u32[]{:S(2)}) collective-permute-start(f32[1,384]{1,0:T(1,128)S(1)} %pad_maximum_fusion.6), channel_id=1, source_target_pairs={{0,2},{1,3},{2,0},{3,1},{8,10},{9,11},{10,8},{11,9},{16,18},{17,19... | collective-permute-start | bytes 4616 | tf_op jit(solution)/shard_map/ppermute | solution.py:39
  344.4 2.5 collective-permute-start.22
  346.9 4.0 %collective-permute-start.23 = (f32[1,384]{1,0:T(1,128)S(1)}, f32[1,384]{1,0:T(1,128)S(1)}, u32[]{:S(2)}, u32[]{:S(2)}) collective-permute-start(f32[1,384]{1,0:T(1,128)S(1)} %pad_maximum_fusion.8), channel_id=1, source_target_pairs={{0,16},{1,17},{2,18},{3,19},{8,24},{9,25},{10,26},{11,27},{16,0},{... | collective-permute-start | bytes 4616 | tf_op jit(solution)/shard_map/ppermute | solution.py:39
  351.0 2.5 collective-permute-start.24
  353.5 4.0 %collective-permute-start.25 = (f32[1,384]{1,0:T(1,128)S(1)}, f32[1,384]{1,0:T(1,128)S(1)}, u32[]{:S(2)}, u32[]{:S(2)}) collective-permute-start(f32[1,384]{1,0:T(1,128)S(1)} %pad_maximum_fusion.10), channel_id=1, source_target_pairs={{0,64},{1,65},{2,66},{3,67},{8,72},{9,73},{10,74},{11,75},{16,80},... | collective-permute-start | bytes 4616 | tf_op jit(solution)/shard_map/ppermute | solution.py:39
Sparse Core Ops, SparseCore 0:
  11.6 47.4 all-gather.3
  127.1 61.0 all-reduce.2
  215.8 29.0 all-reduce.4
  315.6 19.7 reduce-scatter.1

commit v2 on v1

--- a/solution.py
+++ b/solution.py
@@ -65,6 +65,15 @@
         packed = jnp.concatenate(combine(split(keep), split(other)), axis=-1)
         step //= 2
     return split(packed)
+
+
+def butterfly_sum(value, axes, count):
+    step = 1
+    while step < count:
+        pairs = [(i, i ^ step) for i in range(count)]
+        value = value + lax.ppermute(value, axes, pairs)
+        step *= 2
+    return value
 
 
 def halving_scatter(value, axes, count):
@@ -232,7 +241,9 @@
         w_out_all,
         preferred_element_type=jnp.float32,
     )
-    own_mid = hidden_in.astype(jnp.float32) + lax.psum(partial_out, ("row", "col"))
+    own_mid = hidden_in.astype(jnp.float32) + butterfly_sum(
+        partial_out, ("row", "col"), lax.axis_size("row") * lax.axis_size("col")
+    )
     own_normed = rms_scale(own_mid, ffn_gain).astype(jnp.bfloat16)
     normed_mid = doubling_gather(own_normed, "seq", seq_count)
     router = jnp.dot(normed_mid.astype(jnp.float32), w_router, precision=lax.Precision.HIGHEST)
@@ -261,7 +272,7 @@
     gate_part = jnp.einsum(
         "ecd,edgf->ecgf", expert_rows, w_gate_up, preferred_element_type=jnp.float32
     )
-    gate_both = lax.psum(gate_part, "row")
+    gate_both = butterfly_sum(gate_part, "row", lax.axis_size("row"))
     expert_hidden = (jax.nn.silu(gate_both[:, :, 0]) * gate_both[:, :, 1]).astype(jnp.bfloat16)
     expert_result = jnp.einsum(
         "ecf,efd->ecd", expert_hidden, w_down, preferred_element_type=jnp.float32
@@ -280,11 +291,10 @@
     normed_out = doubling_gather(normed_block, ("seq", "col"), block_count)
     vocab_dev = w_head.shape[1]
     row_count = total_rows // lax.axis_size("row")
-    logits = lax.psum_scatter(
+    logits = halving_scatter(
         jnp.dot(normed_out, w_head, preferred_element_type=jnp.float32),
         "row",
-        scatter_dimension=0,
-        tiled=True,
+        lax.axis_size("row"),
     )
     own_targets = lax.dynamic_slice_in_dim(targets, row_index * row_count, row_count, 0)
     vocab_start = block_index * vocab_dev

time: 375 us -> 298 us (0.79)
  waiting for transfers between devices: 177 us -> 99 us
  starting transfers between devices: 50.3 us -> 57.3 us
    psum x2 -> x0, waiting for transfers between devices: 82.8 us -> none  [the longest x1 60.7 us: on_device(): lax.psum(partial_out, ('row', 'col'))]
    reduce_scatter x1 -> x0, waiting for transfers between devices: 19.8 us -> none  [on_device(): lax.psum_scatter(jnp.dot(normed_out, w_head, preferred_element_type=jnp.f...]
    ppermute x0 -> x4, starting transfers between devices: none -> 16.6 us  [butterfly_sum(): value = value + lax.ppermute(value, axes, pairs)]
    ppermute x6 -> x7, waiting for transfers between devices: 19.8 us -> 26.7 us  [halving_scatter(): value = keep + lax.ppermute(send, axes, pairs)]
    ppermute x10, starting transfers between devices: 21.2 us -> 14.6 us  [doubling_gather(): other = lax.ppermute(value, axes, pairs)]
    ppermute x10, waiting for transfers between devices: 23.6 us -> 29.7 us  [doubling_gather(): other = lax.ppermute(value, axes, pairs)]
    ppermute x6, starting transfers between devices: 13 us -> 7.6 us  [butterfly_merge(): other = lax.ppermute(packed, axes, pairs)]
    ppermute x6, waiting for transfers between devices: 6.53 us -> 12 us  [butterfly_merge(): other = lax.ppermute(packed, axes, pairs)]
  transfers between devices with their start and end apart: 30 -> 32, of which waited for: 29 -> 30; matrix products, arithmetic and copies ran while one was open for 12% -> 15% of each run, Pallas kernels for 0% -> 0%
where the time goes in v2:
time: 298 us; the launch traced here: 297 us
  waiting for transfers between devices  99 us (33%)
  local copies, waits for them, and re-layouts  63.1 us (21%)
  starting transfers between devices  57.3 us (19%)
  matrix products  28.9 us (10%)
  blocking collectives  17.2 us (6%)
  other arithmetic  16.7 us (6%)
  between operations  14.8 us (5%)
    unnamed x23, local copies, waits for them, and re-layouts  33 us
    ppermute x10, waiting for transfers between devices, doubling_gather(): other = lax.ppermute(value, axes, pairs)  29.7 us
    ppermute x7, waiting for transfers between devices, halving_scatter(): value = keep + lax.ppermute(send, axes, pairs)  26.7 us
    ppermute x4, starting transfers between devices, butterfly_sum(): value = value + lax.ppermute(value, axes, pairs)  16.6 us
    ppermute x7, starting transfers between devices, halving_scatter(): value = keep + lax.ppermute(send, axes, pairs)  15.6 us
    all_gather x1, waiting for transfers between devices, on_device(): packed = lax.all_gather(jnp.concatenate(pieces), 'seq', axis=0, tiled=False)  15.3 us
    ppermute x10, starting transfers between devices, doubling_gather(): other = lax.ppermute(value, axes, pairs)  14.6 us
    dot_general x1, matrix products, on_device(): jnp.einsum('rqp,rpd->rqd', old_weights, cached_values, precision=lax.Prec...  12.9 us
  transfers between devices with their start and end apart: 32, of which 30 were waited for; matrix products, arithmetic and copies ran while one was open for 15% of the time, Pallas kernels for 0%

profile of v2, /device:TPU:1, one launch (start us, length us, event | category | flops | bytes accessed | tf_op | source)
XLA Modules:
  0.0 296.8 jit_solution(5626185889484225167)
XLA Ops:
  10.1 1.4 pad_maximum_fusion.1
  12.3 31.4 %copy.74 = bf16[64,1536,128]{1,2,0:T(8,128)(2,1)} copy(bf16[64,1536,128]{2,1,0:T(8,128)(2,1)} %param.20) | data formatting | bytes 50331648 | tf_op args[5]
  43.9 15.3 %all-gather.4.cloned.1.call-done = bf16[1179648]{0:T(1024)(128)(2,1)} async-done(((bf16[73728]{0:T(1024)(128)(2,1)}), bf16[1179648]{0:T(1024)(128)(2,1)}) %all-gather.4.cloned.1.call-update) | async-done | bytes 2359312 | tf_op jit(solution)/shard_map/all_gather | solution.py:172
  59.2 3.3 %reshape.384 = bf16[16,73728]{1,0:T(8,128)(2,1)} reshape(bf16[1179648]{0:T(1024)(128)(2,1)} %all-gather.4.cloned.1.call-done) | data formatting | bytes 4718592 | tf_op jit(solution)/shard_map/all_gather | solution.py:172
  62.5 1.2 convert_multiply_fusion.1
  63.7 2.4 fusion.63
  66.1 1.4 mul.287
  67.5 1.6 reduce_sum.81
  70.3 2.3 fusion.10
  72.6 1.5 convert_element_type.69
  74.1 2.9 reshape.331
  77.0 2.2 fusion.66
  81.2 1.3 convolution_convert_fusion
  83.4 8.2 %fusion.2 = (f32[64,12]{1,0:T(8,128)S(1)}, f32[64,12,1536]{2,1,0:T(8,128)S(1)}) fusion(pred[64,1536]{1,0:T(8,128)(4,1)S(1)} %broadcast_compare_fusion, f32[64,12,64]{2,1,0:T(8,128)S(1)} %reshape.332, bf16[64,1536,2,64]{1,3,2,0:T(8,128)(2,1)} %bitcast.65), kind=kOutput, calls=%fused_computation.11 | convolution fusion | flops 909507840 | bytes 17599488 | tf_op jit(solution)/shard_map/rqd,rpd->rqp/dot_general | solution.py:210
  91.6 12.9 %fusion = f32[64,12,64]{2,1,0:T(8,128)S(1)} fusion(bf16[64,1536,2,64]{1,3,2,0:T(8,128)(2,1)} %bitcast.66, f32[64,12,1536]{2,1,0:T(8,128)S(1)} %get-tuple-element.55, f32[64,12]{1,0:T(8,128)S(1)} %max.37, pred[64,1536]{1,0:T(8,128)(4,1)S(1)} %broadcast_compare_fusion), kind=kOutput, calls=%fused_computation.6 | convolution fusion | flops 910688256 | bytes 17599488 | tf_op jit(solution)/shard_map/rqp,rpd->rqd/dot_general | solution.py:229
  104.5 2.4 fusion.3
  108.1 1.3 collective-permute-start
  109.4 4.0 %collective-permute-done = f32[32,792]{1,0:T(8,128)S(1)} collective-permute-done((f32[32,792]{1,0:T(8,128)S(1)}, f32[32,792]{1,0:T(8,128)S(1)}, u32[]{:S(2)}, u32[]{:S(2)}) %collective-permute-start) | collective-permute-done | bytes 101408 | tf_op jit(solution)/shard_map/ppermute | solution.py:64
  114.4 2.8 collective-permute-done.1
  118.6 3.6 %collective-permute-done.2 = f32[8,792]{1,0:T(8,128)S(1)} collective-permute-done((f32[8,792]{1,0:T(8,128)S(1)}, f32[8,792]{1,0:T(8,128)S(1)}, u32[]{:S(2)}, u32[]{:S(2)}) %collective-permute-start.2) | collective-permute-done | bytes 25376 | tf_op jit(solution)/shard_map/ppermute | solution.py:64
  127.5 2.3 collective-permute-done.4
  129.8 2.8 collective-permute-start.5
  132.6 2.3 collective-permute-done.5
  134.9 8.8 %collective-permute-start.6 = (f32[16,1536]{1,0:T(8,128)S(1)}, f32[16,1536]{1,0:T(8,128)S(1)}, u32[]{:S(2)}, u32[]{:S(2)}) collective-permute-start(f32[16,1536]{1,0:T(8,128)S(1)} %add.320), channel_id=1, source_target_pairs={{0,4},{1,5},{2,6},{3,7},{4,0},{5,1},{6,2},{7,3},{8,12},{9,13},{10,... | collective-permute-start | bytes 294920 | tf_op jit(solution)/shard_map/ppermute | solution.py:74
  145.9 1.9 collective-permute-done.7
  147.9 2.3 collective-permute-start.8
  150.5 2.4 collective-permute-done.8
  153.9 1.4 scatter_custom_fusion
  155.4 2.2 collective-permute-done.9
  157.6 1.9 collective-permute-start.10
  160.2 7.7 %collective-permute-done.10 = bf16[128,1536]{1,0:T(8,128)(2,1)S(1)} collective-permute-done((bf16[128,1536]{1,0:T(8,128)(2,1)S(1)}, bf16[128,1536]{1,0:T(8,128)(2,1)S(1)}, u32[]{:S(2)}, u32[]{:S(2)}) %collective-permute-start.10) | collective-permute-done | bytes 393248 | tf_op jit(solution)/shard_map/ppermute | solution.py:100
  168.8 1.4 convolution_bitcast_fusion
  170.2 3.8 %collective-permute-start.11 = (f32[1,64,2,256]{3,1,2,0:T(8,128)S(1)}, f32[1,64,2,256]{3,1,2,0:T(8,128)S(1)}, u32[]{:S(2)}, u32[]{:S(2)}) collective-permute-start(f32[1,64,2,256]{3,1,2,0:T(8,128)S(1)} %convolution_bitcast_fusion), channel_id=1, source_target_pairs={{0,4},{4,0},{1,5},{5,1},{2,6},{6,2},{3,7},{7,3},{8,12},{12,8},{9,1... | collective-permute-start | bytes 393224 | tf_op jit(solution)/shard_map/ppermute | solution.py:74
  174.7 4.8 %gather_fusion.2 = f32[512]{0:T(512)S(1)} fusion(f32[256,16]{0,1:T(8,128)S(1)} %fusion.68, s32[512]{0:T(512)S(1)} %reshape.362), kind=kCustom, calls=%fused_computation.2 | custom fusion | bytes 8192 | tf_op jit(solution)/shard_map/jit(take_along_axis)/gather | solution.py:250
  184.1 11.0 %collective-permute-done.12 = f32[128,768]{1,0:T(8,128)S(1)} collective-permute-done((f32[128,768]{1,0:T(8,128)S(1)}, f32[128,768]{1,0:T(8,128)S(1)}, u32[]{:S(2)}, u32[]{:S(2)}) %collective-permute-start.12) | collective-permute-done | bytes 393248 | tf_op jit(solution)/shard_map/ppermute | solution.py:89
  195.4 5.5 %collective-permute-done.13 = f32[64,768]{1,0:T(8,128)S(1)} collective-permute-done((f32[64,768]{1,0:T(8,128)S(1)}, f32[64,768]{1,0:T(8,128)S(1)}, u32[]{:S(2)}, u32[]{:S(2)}) %collective-permute-start.13) | collective-permute-done | bytes 196640 | tf_op jit(solution)/shard_map/ppermute | solution.py:89
  200.9 1.8 collective-permute-start.14
  202.8 3.2 %collective-permute-done.14 = f32[32,768]{1,0:T(8,128)S(1)} collective-permute-done((f32[32,768]{1,0:T(8,128)S(1)}, f32[32,768]{1,0:T(8,128)S(1)}, u32[]{:S(2)}, u32[]{:S(2)}) %collective-permute-start.14) | collective-permute-done | bytes 98336 | tf_op jit(solution)/shard_map/ppermute | solution.py:89
  206.5 2.6 collective-permute-done.15
  209.1 2.8 collective-permute-start.16
  211.9 1.5 collective-permute-done.16
  213.4 1.3 collective-permute-start.17
  214.7 1.3 collective-permute-done.17
  216.2 8.5 %psum.7 = f32[4]{0:T(128)S(1)} all-reduce(f32[4]{0:T(128)S(1)} %get-tuple-element.16), channel_id=1, replica_groups=mesh['seq'=16,'row'=2,'col'=4] {'row'}, use_global_device_ids=true, to_apply=%region_14.15 | all-reduce | flops 4 | bytes 32 | tf_op jit(solution)/shard_map/psum | solution.py:125
  226.4 1.3 collective-permute-done.18
  227.7 2.8 collective-permute-start.19
  230.5 1.4 collective-permute-done.19
  232.3 2.3 collective-permute-done.20
  234.6 2.0 collective-permute-start.21
  236.5 2.6 collective-permute-done.21
  239.3 3.7 %collective-permute-done.22 = bf16[64,768]{1,0:T(8,128)(2,1)S(1)} collective-permute-done((bf16[64,768]{1,0:T(8,128)(2,1)S(1)}, bf16[64,768]{1,0:T(8,128)(2,1)S(1)}, u32[]{:S(2)}, u32[]{:S(2)}) %collective-permute-start.22) | collective-permute-done | bytes 98336 | tf_op jit(solution)/shard_map/ppermute | solution.py:100
  243.0 2.0 collective-permute-start.23
  245.0 4.4 %collective-permute-done.23 = bf16[128,768]{1,0:T(8,128)(2,1)S(1)} collective-permute-done((bf16[128,768]{1,0:T(8,128)(2,1)S(1)}, bf16[128,768]{1,0:T(8,128)(2,1)S(1)}, u32[]{:S(2)}, u32[]{:S(2)}) %collective-permute-start.23) | collective-permute-done | bytes 196640 | tf_op jit(solution)/shard_map/ppermute | solution.py:100
  250.0 7.9 %collective-permute-start.24 = (f32[128,1024]{1,0:T(8,128)S(1)}, f32[128,1024]{1,0:T(8,128)}, u32[]{:S(2)}, u32[]{:S(2)}) collective-permute-start(f32[128,1024]{1,0:T(8,128)S(1)} %slice_select_fusion), channel_id=1, source_target_pairs={{0,4},{4,0},{1,5},{5,1},{2,6},{6,2},{3,7},{7,3},{8,12},{12,8},{9,1... | collective-permute-start | bytes 1572872 | tf_op jit(solution)/shard_map/ppermute | solution.py:89
  257.9 1.6 collective-permute-done.24
  261.0 1.3 collective-permute-start.25
  262.3 1.2 collective-permute-done.25
  263.5 2.8 collective-permute-start.26
  268.0 2.0 collective-permute-done.27
  271.3 2.8 collective-permute-done.28
  274.2 2.4 collective-permute-done.29
  276.7 1.8 collective-permute-start.30
  278.5 2.2 collective-permute-done.30
  280.7 8.7 %all-gather.1 = f32[1,256]{1,0:T(1,128)S(1)} all-gather(f32[1,128]{1,0:T(1,128)S(1)} %fusion.43), channel_id=3, replica_groups=mesh['seq'=16,'row'=2,'col'=4] {'row'}, dimensions={1}, use_global_device_ids=true | all-gather | bytes 1536 | tf_op jit(solution)/shard_map/all_gather | solution.py:315
  (179 shorter events, 36.4 us)
Async XLA Ops:
  7.2 242.2 %copy-start = (bf16[768,1024]{1,0:T(8,128)(2,1)S(1)}, bf16[768,1024]{1,0:T(8,128)(2,1)}, u32[]{:S(2)}) copy-start(bf16[768,1024]{1,0:T(8,128)(2,1)} %param.28) | copy-start | bytes 4718596
  7.2 52.0 %all-gather.4.cloned.1.call-start = ((), (), s32[]{:S(2)}) async-start(), calls=%async_computation | async-start | bytes 2506752 | tf_op jit(solution)/shard_map/all_gather | solution.py:172
  12.3 31.5 %copy-start.8 = (s32[64]{0:T(128)S(1)}, s32[64]{0:T(128)}, u32[]{:S(2)}) copy-start(s32[64]{0:T(128)} %param.21) | copy-start | bytes 772
  69.4 10.8 %slice-start = ((bf16[16,73728]{1,0:T(8,128)(2,1)}), bf16[16,12288]{1,0:T(8,128)(2,1)S(1)}, s32[]{:S(2)}) async-start(bf16[16,73728]{1,0:T(8,128)(2,1)} %reshape.384), calls=%async_computation.1 | async-start | bytes 786432 | tf_op jit(solution)/shard_map/slice | solution.py:176
  104.5 18.8 %copy-start.1 = (bf16[16,18432]{1,0:T(8,128)(2,1)S(1)}, bf16[16,18432]{1,0:T(8,128)(2,1)}, u32[]{:S(2)}) copy-start(bf16[16,18432]{1,0:T(8,128)(2,1)} %get-tuple-element.35) | copy-start | bytes 1769476
  107.1 20.4 %copy-start.5 = (s32[256,2]{0,1:T(2,128)S(1)}, s32[256,2]{0,1:T(2,128)}, u32[]{:S(2)}) copy-start(s32[256,2]{0,1:T(2,128)} %param.24) | copy-start | bytes 6148
  107.8 36.8 %copy-start.3 = (bf16[16,1536]{1,0:T(8,128)(2,1)S(1)}, bf16[16,1536]{1,0:T(8,128)(2,1)}, u32[]{:S(2)}) copy-start(bf16[16,1536]{1,0:T(8,128)(2,1)} %param.15) | copy-start | bytes 147460
  107.8 37.0 %copy-start.6 = (f32[1536]{0:T(1024)S(1)}, f32[1536]{0:T(1024)}, u32[]{:S(2)}) copy-start(f32[1536]{0:T(1024)} %param.22) | copy-start | bytes 18436
  108.1 5.2 %collective-permute-start = (f32[32,792]{1,0:T(8,128)S(1)}, f32[32,792]{1,0:T(8,128)S(1)}, u32[]{:S(2)}, u32[]{:S(2)}) collective-permute-start(f32[32,792]{1,0:T(8,128)S(1)} %get-tuple-element.38), channel_id=1, source_target_pairs={{0,64},{8,72},{16,80},{24,88},{32,96},{40,104},{48,112},{56,120},{... | collective-permute-start | bytes 304136 | tf_op jit(solution)/shard_map/ppermute | solution.py:64
  114.1 3.1 %collective-permute-start.1 = (f32[16,792]{1,0:T(8,128)S(1)}, f32[16,792]{1,0:T(8,128)S(1)}, u32[]{:S(2)}, u32[]{:S(2)}) collective-permute-start(f32[16,792]{1,0:T(8,128)S(1)} %get-tuple-element.42), channel_id=1, source_target_pairs={{0,32},{8,40},{16,48},{24,56},{32,0},{40,8},{48,16},{56,24},{64,96... | collective-permute-start | bytes 152072 | tf_op jit(solution)/shard_map/ppermute | solution.py:64
  117.9 4.3 %collective-permute-start.2 = (f32[8,792]{1,0:T(8,128)S(1)}, f32[8,792]{1,0:T(8,128)S(1)}, u32[]{:S(2)}, u32[]{:S(2)}) collective-permute-start(f32[8,792]{1,0:T(8,128)S(1)} %get-tuple-element.44), channel_id=1, source_target_pairs={{0,16},{8,24},{16,0},{24,8},{32,48},{40,56},{48,32},{56,40},{64,80... | collective-permute-start | bytes 76040 | tf_op jit(solution)/shard_map/ppermute | solution.py:64
  122.7 51.3 %copy-start.4 = (f32[1536,16]{0,1:T(8,128)S(1)}, f32[1536,16]{0,1:T(8,128)}, u32[]{:S(2)}) copy-start(f32[1536,16]{0,1:T(8,128)} %param.23) | copy-start | bytes 294916
  122.8 2.9 collective-permute-start.3
  126.3 3.5 %collective-permute-start.4 = (f32[16,1536]{1,0:T(8,128)S(1)}, f32[16,1536]{1,0:T(8,128)S(1)}, u32[]{:S(2)}, u32[]{:S(2)}) collective-permute-start(f32[16,1536]{1,0:T(8,128)S(1)} %fusion.67), channel_id=1, source_target_pairs={{0,1},{1,0},{2,3},{3,2},{4,5},{5,4},{6,7},{7,6},{8,9},{9,8},{10,11... | collective-permute-start | bytes 294920 | tf_op jit(solution)/shard_map/ppermute | solution.py:74
  129.8 5.1 %collective-permute-start.5 = (f32[16,1536]{1,0:T(8,128)S(1)}, f32[16,1536]{1,0:T(8,128)S(1)}, u32[]{:S(2)}, u32[]{:S(2)}) collective-permute-start(f32[16,1536]{1,0:T(8,128)S(1)} %add.319), channel_id=1, source_target_pairs={{0,2},{1,3},{2,0},{3,1},{4,6},{5,7},{6,4},{7,5},{8,10},{9,11},{10,... | collective-permute-start | bytes 294920 | tf_op jit(solution)/shard_map/ppermute | solution.py:74
  134.9 9.7 %collective-permute-start.6 = (f32[16,1536]{1,0:T(8,128)S(1)}, f32[16,1536]{1,0:T(8,128)S(1)}, u32[]{:S(2)}, u32[]{:S(2)}) collective-permute-start(f32[16,1536]{1,0:T(8,128)S(1)} %add.320), channel_id=1, source_target_pairs={{0,4},{1,5},{2,6},{3,7},{4,0},{5,1},{6,2},{7,3},{8,12},{9,13},{10,... | collective-permute-start | bytes 294920 | tf_op jit(solution)/shard_map/ppermute | solution.py:74
  144.8 3.0 %collective-permute-start.7 = (bf16[16,1536]{1,0:T(8,128)(2,1)S(1)}, bf16[16,1536]{1,0:T(8,128)(2,1)S(1)}, u32[]{:S(2)}, u32[]{:S(2)}) collective-permute-start(bf16[16,1536]{1,0:T(8,128)(2,1)S(1)} %multiply_convert_fusion), channel_id=1, source_target_pairs={{0,8},{8,0},{16,24},{24,16},{32,40},{40,32},{48,56},{56,48},{64,72... | collective-permute-start | bytes 147464 | tf_op jit(solution)/shard_map/ppermute | solution.py:100
  147.9 5.1 %collective-permute-start.8 = (bf16[32,1536]{1,0:T(8,128)(2,1)S(1)}, bf16[32,1536]{1,0:T(8,128)(2,1)S(1)}, u32[]{:S(2)}, u32[]{:S(2)}) collective-permute-start(bf16[32,1536]{1,0:T(8,128)(2,1)S(1)} %maximum_select_fusion.6), channel_id=1, source_target_pairs={{0,16},{8,24},{16,0},{24,8},{32,48},{40,56},{48,32},{56,40},{64,80... | collective-permute-start | bytes 294920 | tf_op jit(solution)/shard_map/ppermute | solution.py:100
  152.9 4.6 %collective-permute-start.9 = (bf16[64,1536]{1,0:T(8,128)(2,1)S(1)}, bf16[64,1536]{1,0:T(8,128)(2,1)S(1)}, u32[]{:S(2)}, u32[]{:S(2)}) collective-permute-start(bf16[64,1536]{1,0:T(8,128)(2,1)S(1)} %maximum_select_fusion.4), channel_id=1, source_target_pairs={{0,32},{8,40},{16,48},{24,56},{32,0},{40,8},{48,16},{56,24},{64,96... | collective-permute-start | bytes 589832 | tf_op jit(solution)/shard_map/ppermute | solution.py:100
  157.6 10.2 %collective-permute-start.10 = (bf16[128,1536]{1,0:T(8,128)(2,1)S(1)}, bf16[128,1536]{1,0:T(8,128)(2,1)S(1)}, u32[]{:S(2)}, u32[]{:S(2)}) collective-permute-start(bf16[128,1536]{1,0:T(8,128)(2,1)S(1)} %maximum_select_fusion.1), channel_id=1, source_target_pairs={{0,64},{8,72},{16,80},{24,88},{32,96},{40,104},{48,112},{56,120},{... | collective-permute-start | bytes 1179656 | tf_op jit(solution)/shard_map/ppermute | solution.py:100
  170.2 11.2 %collective-permute-start.11 = (f32[1,64,2,256]{3,1,2,0:T(8,128)S(1)}, f32[1,64,2,256]{3,1,2,0:T(8,128)S(1)}, u32[]{:S(2)}, u32[]{:S(2)}) collective-permute-start(f32[1,64,2,256]{3,1,2,0:T(8,128)S(1)} %convolution_bitcast_fusion), channel_id=1, source_target_pairs={{0,4},{4,0},{1,5},{5,1},{2,6},{6,2},{3,7},{7,3},{8,12},{12,8},{9,1... | collective-permute-start | bytes 393224 | tf_op jit(solution)/shard_map/ppermute | solution.py:74
  174.7 6.7 %copy-start.2 = (bf16[1,256,768]{2,1,0:T(8,128)(2,1)S(1)}, bf16[1,256,768]{2,1,0:T(8,128)(2,1)}, u32[]{:S(2)}) copy-start(bf16[1,256,768]{2,1,0:T(8,128)(2,1)} %param.26) | copy-start | bytes 1179652
  179.5 35.1 %copy-start.7 = (f32[1536]{0:T(1024)S(1)}, f32[1536]{0:T(1024)}, u32[]{:S(2)}) copy-start(f32[1536]{0:T(1024)} %param.27) | copy-start | bytes 18436
  181.6 76.3 %copy-start.9 = (s32[256]{0:T(256)S(1)}, s32[256]{0:T(256)}, u32[]{:S(2)}) copy-start(s32[256]{0:T(256)} %param.29) | copy-start | bytes 3076
  182.9 12.2 %collective-permute-start.12 = (f32[128,768]{1,0:T(8,128)S(1)}, f32[128,768]{1,0:T(8,128)S(1)}, u32[]{:S(2)}, u32[]{:S(2)}) collective-permute-start(f32[128,768]{1,0:T(8,128)S(1)} %slice_select_fusion.1), channel_id=1, source_target_pairs={{0,64},{1,65},{2,66},{3,67},{8,72},{9,73},{10,74},{11,75},{16,80},... | collective-permute-start | bytes 1179656 | tf_op jit(solution)/shard_map/ppermute | solution.py:89
  195.2 5.7 %collective-permute-start.13 = (f32[64,768]{1,0:T(8,128)S(1)}, f32[64,768]{1,0:T(8,128)S(1)}, u32[]{:S(2)}, u32[]{:S(2)}) collective-permute-start(f32[64,768]{1,0:T(8,128)S(1)} %slice_select_fusion.2), channel_id=1, source_target_pairs={{0,32},{1,33},{2,34},{3,35},{8,40},{9,41},{10,42},{11,43},{16,48},... | collective-permute-start | bytes 589832 | tf_op jit(solution)/shard_map/ppermute | solution.py:89
  200.9 5.1 %collective-permute-start.14 = (f32[32,768]{1,0:T(8,128)S(1)}, f32[32,768]{1,0:T(8,128)S(1)}, u32[]{:S(2)}, u32[]{:S(2)}) collective-permute-start(f32[32,768]{1,0:T(8,128)S(1)} %slice_select_fusion.5), channel_id=1, source_target_pairs={{0,16},{1,17},{2,18},{3,19},{8,24},{9,25},{10,26},{11,27},{16,0},{... | collective-permute-start | bytes 294920 | tf_op jit(solution)/shard_map/ppermute | solution.py:89
  206.0 3.0 %collective-permute-start.15 = (f32[16,768]{1,0:T(8,128)S(1)}, f32[16,768]{1,0:T(8,128)S(1)}, u32[]{:S(2)}, u32[]{:S(2)}) collective-permute-start(f32[16,768]{1,0:T(8,128)S(1)} %slice_select_fusion.8), channel_id=1, source_target_pairs={{0,8},{1,9},{2,10},{3,11},{8,0},{9,1},{10,2},{11,3},{16,24},{17,25... | collective-permute-start | bytes 147464 | tf_op jit(solution)/shard_map/ppermute | solution.py:89
  209.1 4.3 %collective-permute-start.16 = (f32[8,768]{1,0:T(8,128)S(1)}, f32[8,768]{1,0:T(8,128)S(1)}, u32[]{:S(2)}, u32[]{:S(2)}) collective-permute-start(f32[8,768]{1,0:T(8,128)S(1)} %slice_select_fusion.11), channel_id=1, source_target_pairs={{0,2},{1,3},{2,0},{3,1},{8,10},{9,11},{10,8},{11,9},{16,18},{17,19... | collective-permute-start | bytes 73736 | tf_op jit(solution)/shard_map/ppermute | solution.py:89
  213.4 2.6 collective-permute-start.17
  225.2 2.5 collective-permute-start.18
  227.7 4.1 %collective-permute-start.19 = (bf16[8,768]{1,0:T(8,128)(2,1)S(1)}, bf16[8,768]{1,0:T(8,128)(2,1)S(1)}, u32[]{:S(2)}, u32[]{:S(2)}) collective-permute-start(bf16[8,768]{1,0:T(8,128)(2,1)S(1)} %maximum_select_fusion.10), channel_id=1, source_target_pairs={{0,2},{1,3},{2,0},{3,1},{8,10},{9,11},{10,8},{11,9},{16,18},{17,19... | collective-permute-start | bytes 36872 | tf_op jit(solution)/shard_map/ppermute | solution.py:100
  231.9 2.7 collective-permute-start.20
  234.6 4.5 %collective-permute-start.21 = (bf16[32,768]{1,0:T(8,128)(2,1)S(1)}, bf16[32,768]{1,0:T(8,128)(2,1)S(1)}, u32[]{:S(2)}, u32[]{:S(2)}) collective-permute-start(bf16[32,768]{1,0:T(8,128)(2,1)S(1)} %maximum_select_fusion.8), channel_id=1, source_target_pairs={{0,16},{1,17},{2,18},{3,19},{8,24},{9,25},{10,26},{11,27},{16,0},{... | collective-permute-start | bytes 147464 | tf_op jit(solution)/shard_map/ppermute | solution.py:100
  239.1 3.8 %collective-permute-start.22 = (bf16[64,768]{1,0:T(8,128)(2,1)S(1)}, bf16[64,768]{1,0:T(8,128)(2,1)S(1)}, u32[]{:S(2)}, u32[]{:S(2)}) collective-permute-start(bf16[64,768]{1,0:T(8,128)(2,1)S(1)} %maximum_select_fusion.7), channel_id=1, source_target_pairs={{0,32},{1,33},{2,34},{3,35},{8,40},{9,41},{10,42},{11,43},{16,48},... | collective-permute-start | bytes 294920 | tf_op jit(solution)/shard_map/ppermute | solution.py:100
  243.0 6.3 %collective-permute-start.23 = (bf16[128,768]{1,0:T(8,128)(2,1)S(1)}, bf16[128,768]{1,0:T(8,128)(2,1)S(1)}, u32[]{:S(2)}, u32[]{:S(2)}) collective-permute-start(bf16[128,768]{1,0:T(8,128)(2,1)S(1)} %maximum_select_fusion.5), channel_id=1, source_target_pairs={{0,64},{1,65},{2,66},{3,67},{8,72},{9,73},{10,74},{11,75},{16,80},... | collective-permute-start | bytes 589832 | tf_op jit(solution)/shard_map/ppermute | solution.py:100
  250.0 9.5 %collective-permute-start.24 = (f32[128,1024]{1,0:T(8,128)S(1)}, f32[128,1024]{1,0:T(8,128)}, u32[]{:S(2)}, u32[]{:S(2)}) collective-permute-start(f32[128,1024]{1,0:T(8,128)S(1)} %slice_select_fusion), channel_id=1, source_target_pairs={{0,4},{4,0},{1,5},{5,1},{2,6},{6,2},{3,7},{7,3},{8,12},{12,8},{9,1... | collective-permute-start | bytes 1572872 | tf_op jit(solution)/shard_map/ppermute | solution.py:89
  261.0 2.5 collective-permute-start.25
  263.5 4.0 %collective-permute-start.26 = (f32[1,384]{1,0:T(1,128)S(1)}, f32[1,384]{1,0:T(1,128)S(1)}, u32[]{:S(2)}, u32[]{:S(2)}) collective-permute-start(f32[1,384]{1,0:T(1,128)S(1)} %pad_maximum_fusion.6), channel_id=1, source_target_pairs={{0,2},{1,3},{2,0},{3,1},{8,10},{9,11},{10,8},{11,9},{16,18},{17,19... | collective-permute-start | bytes 4616 | tf_op jit(solution)/shard_map/ppermute | solution.py:39
  267.6 2.5 collective-permute-start.27
  270.1 4.0 %collective-permute-start.28 = (f32[1,384]{1,0:T(1,128)S(1)}, f32[1,384]{1,0:T(1,128)S(1)}, u32[]{:S(2)}, u32[]{:S(2)}) collective-permute-start(f32[1,384]{1,0:T(1,128)S(1)} %pad_maximum_fusion.8), channel_id=1, source_target_pairs={{0,16},{1,17},{2,18},{3,19},{8,24},{9,25},{10,26},{11,27},{16,0},{... | collective-permute-start | bytes 4616 | tf_op jit(solution)/shard_map/ppermute | solution.py:39
  274.1 2.5 collective-permute-start.29
  276.7 4.0 %collective-permute-start.30 = (f32[1,384]{1,0:T(1,128)S(1)}, f32[1,384]{1,0:T(1,128)S(1)}, u32[]{:S(2)}, u32[]{:S(2)}) collective-permute-start(f32[1,384]{1,0:T(1,128)S(1)} %pad_maximum_fusion.10), channel_id=1, source_target_pairs={{0,64},{1,65},{2,66},{3,67},{8,72},{9,73},{10,74},{11,75},{16,80},... | collective-permute-start | bytes 4616 | tf_op jit(solution)/shard_map/ppermute | solution.py:39
Sparse Core Ops, SparseCore 0:
  11.6 47.4 all-gather.3
